TPU v7x, 128 devices: a whole 4x4x4 slice. The times are simulated.
128 devices in a mesh: rows: 32 (over y, x, z_lo), cols: 4 (over z_hi, core).
Axes of the slice: x: 4, y: 4, z: 4 (z_hi: 2, z_lo: 2; z = z_hi * 2 + z_lo), core: 2. Of those that a mesh axis runs over, the one named last changes fastest.
Arguments:
- block_input: bfloat16 [2, 128, 128, 1536], P(None, 'rows', 'cols'), may hold values from -6 to 6
- token_grads: bfloat16 [2, 4096, 6144], P(None, ('rows', 'cols')), may hold values from -6 to 6
- conv_kernel: float32 [7, 7, 1536], replicated, may hold values from -0.875 to 0.875
- layer_norm_gain: float32 [1536], replicated, may hold values from 0.25 to 1.75
- w_in: bfloat16 [1536, 3072], P('rows', 'cols'), may hold values from -0.15625 to 0.15625
- w_out: bfloat16 [3072, 1536], P('cols', 'rows'), may hold values from -0.109375 to 0.109375
- layer_scale: float32 [1536], replicated, may hold values from 0.25 to 1.75
Outputs:
- input_grad: bfloat16 [2, 128, 128, 1536], P(None, 'rows', 'cols')
- grad_w1: float32 [1536, 3072], P('rows', 'cols')
- grad_w2: float32 [3072, 1536], P('cols', 'rows')
- grad_kernel: float32 [7, 7, 1536], replicated
All inputs are finite; a program needn't handle non-finite values.
Results may differ from a plain program's by a relative error of at most 0.0062.
Values may be sent and summed in bfloat16 or wider, within the bound.
No kernel may reach another device: no remote copies, remote signals or barrier semaphores. Data moves between devices by JAX's collectives and lax.ppermute only.
A program may use at most 128 MiB of HBM per device.

v0:
```python
import jax
import jax.numpy as jnp
from jax import lax
from jax.sharding import PartitionSpec as P


def with_halo(value, sides, width):
    for axis, dim in sides:
        peers, length = (lax.axis_size(axis), value.shape[dim])
        up = [(i, (i + 1) % peers) for i in range(peers - 1)]
        down = [(j, i) for i, j in up]
        last = lax.slice_in_dim(value, length - width, length, axis=dim)
        first = lax.slice_in_dim(value, 0, width, axis=dim)
        before = lax.ppermute(last, axis, up)
        after = lax.ppermute(first, axis, down)
        value = jnp.concatenate([before, value, after], axis=dim)
    return value


def local(block_input, token_grads, conv_kernel, layer_norm_gain, w_in, w_out, layer_scale):
    images, tile_rows, tile_cols, channel_total = block_input.shape
    kernel_size = conv_kernel.shape[0]
    kernel_reach = kernel_size // 2
    n_rows = lax.axis_size("rows")
    n_cols = lax.axis_size("cols")
    run_count = tile_rows // 2
    half_cols = tile_cols // 2
    col_index = lax.axis_index("cols")
    group_rows = lax.all_gather(token_grads, "cols", axis=1, tiled=True)
    group_rows = group_rows.reshape(images, run_count, n_cols, half_cols, 4 * channel_total)
    merged = lax.dynamic_index_in_dim(group_rows, col_index, 2, keepdims=False)
    out_grad = merged.reshape(images, run_count, half_cols, 2, 2, channel_total)
    out_grad = out_grad.transpose(0, 1, 3, 2, 4, 5).reshape(
        images, tile_rows, tile_cols, channel_total
    )
    padded = with_halo(block_input, (("rows", 1), ("cols", 2)), kernel_reach)
    padded = padded.astype(jnp.float32)
    conv_out = jnp.zeros((images, tile_rows, tile_cols, channel_total), jnp.float32)
    for r in range(kernel_size):
        for s in range(kernel_size):
            conv_out = (
                conv_out + conv_kernel[r, s] * padded[:, r : r + tile_rows, s : s + tile_cols]
            )
    mean_val = jnp.mean(conv_out, axis=-1, keepdims=True)
    centered_input = conv_out - mean_val
    var_val = jnp.mean(centered_input * centered_input, axis=-1, keepdims=True)
    inverse_deviation = lax.rsqrt(var_val + 1e-06)
    standardized_input = centered_input * inverse_deviation
    pixel_total = images * tile_rows * tile_cols
    norm_output = (
        (standardized_input * layer_norm_gain)
        .astype(jnp.bfloat16)
        .reshape(pixel_total, channel_total)
    )
    branch_grad = (
        (out_grad.astype(jnp.float32) * layer_scale)
        .astype(jnp.bfloat16)
        .reshape(pixel_total, channel_total)
    )
    branch_all = lax.all_gather(branch_grad, "cols", axis=0, tiled=True)
    normed_all = lax.all_gather(norm_output, "cols", axis=0, tiled=True)
    w_in_cols = lax.all_gather(w_in, "rows", axis=0, tiled=True)
    pre = jnp.dot(normed_all, w_in_cols, preferred_element_type=jnp.float32)
    cdf = 0.5 * (1.0 + lax.erf(pre * 0.7071067811865476))
    hidden = (pre * cdf).astype(jnp.bfloat16)
    back_hidden = lax.dot_general(
        branch_all,
        lax.all_gather(w_out, "rows", axis=1, tiled=True),
        (((1,), (1,)), ((), ())),
        preferred_element_type=jnp.float32,
    )
    density = jnp.exp(-0.5 * pre * pre) * 0.3989422804014327
    hidden_grad = (back_hidden * (cdf + pre * density)).astype(jnp.bfloat16)
    scale = 1.0 / float(images * tile_rows * tile_cols * n_rows * n_cols) ** 0.5
    out_terms = (
        lax.dot_general(
            hidden, branch_all, (((0,), (0,)), ((), ())), preferred_element_type=jnp.float32
        )
        * scale
    )
    grad_w2 = lax.psum_scatter(out_terms, "rows", scatter_dimension=1, tiled=True)
    grad_w1 = lax.psum_scatter(
        lax.dot_general(
            normed_all, hidden_grad, (((0,), (0,)), ((), ())), preferred_element_type=jnp.float32
        )
        * scale,
        "rows",
        scatter_dimension=0,
        tiled=True,
    )
    normed_grad = lax.psum_scatter(
        lax.dot_general(
            hidden_grad, w_in_cols, (((1,), (1,)), ((), ())), preferred_element_type=jnp.float32
        ),
        "cols",
        scatter_dimension=0,
        tiled=True,
    )
    gain_applied = (
        normed_grad.reshape(images, tile_rows, tile_cols, channel_total) * layer_norm_gain
    )
    convolution_gradient = inverse_deviation * (
        gain_applied
        - jnp.mean(gain_applied, axis=-1, keepdims=True)
        - standardized_input * jnp.mean(gain_applied * standardized_input, axis=-1, keepdims=True)
    )
    kernel_rows = []
    for r in range(kernel_size):
        row_terms = []
        for s in range(kernel_size):
            row_terms.append(
                jnp.sum(
                    convolution_gradient * padded[:, r : r + tile_rows, s : s + tile_cols],
                    axis=(0, 1, 2),
                )
            )
        kernel_rows.append(jnp.stack(row_terms))
    kernel_local = jnp.stack(kernel_rows) * scale
    grad_kernel = lax.psum(kernel_local, ("rows", "cols"))
    grad_pad = with_halo(convolution_gradient, (("rows", 1), ("cols", 2)), kernel_reach)
    total = out_grad.astype(jnp.float32)
    for r in range(kernel_size):
        for s in range(kernel_size):
            row_from = 2 * kernel_reach - r
            col_from = 2 * kernel_reach - s
            total = (
                total
                + conv_kernel[r, s]
                * grad_pad[:, row_from : row_from + tile_rows, col_from : col_from + tile_cols]
            )
    input_grad = total.astype(jnp.bfloat16)
    return (input_grad, grad_w1, grad_w2, grad_kernel)


def solution(mesh):
    return jax.shard_map(
        local,
        mesh=mesh,
        in_specs=(
            P(None, "rows", "cols", None),
            P(None, ("rows", "cols"), None),
            P(),
            P(),
            P("rows", "cols"),
            P("cols", "rows"),
            P(),
        ),
        out_specs=(P(None, "rows", "cols", None), P("rows", "cols"), P("cols", "rows"), P()),
        check_vma=False,
    )
```

profile of v0, /device:TPU:1, one launch (start us, length us, event | category | flops | bytes accessed | tf_op | source)
XLA Modules:
  0.0 1040.1 jit_solution(5135954148475976362)
XLA Ops:
  9.0 4.4 collective-permute-start
  16.4 28.9 %collective-permute-done = bf16[2,3,32,1536]{3,0,2,1:T(2,128)(2,1)S(1)} collective-permute-done((bf16[2,3,32,1536]{3,0,2,1:T(2,128)(2,1)S(1)}, bf16[2,3,32,1536]{3,0,2,1:T(2,128)(2,1)S(1)}, u32[]{:S(2)}, u32[]{:S(2)}) %collective-permute-start) | collective-permute-done | bytes 589856 | tf_op jit(solution)/shard_map/ppermute | solution.py:14
  47.3 8.6 collective-permute-start.2
  60.2 4.1 collective-permute-done.3
  64.3 2.9 maximum_convert_fusion
  67.6 55.5 %fusion.66 = (f32[2,4,32]{0,2,1:T(8,128)S(1)}, f32[2,4,32,1536]{3,0,2,1:T(2,128)}) fusion(f32[2,10,38,1536]{3,0,2,1:T(2,128)S(1)} %maximum_convert_fusion, f32[1536]{0:T(1024)S(1)} %copy-done.48, f32[1536]{0:T(1024)S(1)} %copy-done.50, f32[1536]{0:T(1024)S(1)} %get-tuple-element.62, f32[1536]{0:T(1024)S(1)} %get-tuple-element.63, ...), kind=kLoop, calls=%fused_computation.252 | loop fusion | flops 38534912 | bytes 78945280 | tf_op jit(solution)/shard_map/reduce_sum | solution.py:44
  123.2 2.5 multiply_reduce_fusion.51
  132.2 2.4 reshape.111
  136.2 57.2 %all-gather.14.cloned.1.call-done = bf16[1536,768]{1,0:T(8,128)(2,1)} async-done(((bf16[48,768]{1,0:T(8,128)(2,1)}), bf16[1536,768]{1,0:T(8,128)(2,1)}) %all-gather.14.cloned.1.call-update) | async-done | bytes 2359312 | tf_op jit(solution)/shard_map/all_gather | solution.py:62
  193.4 57.3 %all-gather.12.cloned.1.call-done = bf16[1024,1536]{1,0:T(8,128)(2,1)} async-done(((bf16[256,1536]{1,0:T(8,128)(2,1)}), bf16[1024,1536]{1,0:T(8,128)(2,1)}) %all-gather.12.cloned.1.call-update) | async-done | bytes 3145744 | tf_op jit(solution)/shard_map/all_gather | solution.py:61
  250.7 6.9 fusion.70
  257.6 125.3 %all-gather.10.cloned.1.call-done = bf16[768,1536]{0,1:T(8,128)(2,1)} async-done(((bf16[768,48]{0,1:T(8,128)(2,1)}), bf16[768,1536]{0,1:T(8,128)(2,1)}) %all-gather.10.cloned.1.call-update) | async-done | bytes 2359312 | tf_op jit(solution)/shard_map/all_gather | solution.py:68
  382.9 56.0 %all-gather.8.cloned.1.call-done = bf16[1024,1536]{1,0:T(8,128)(2,1)} async-done(((bf16[256,1536]{1,0:T(8,128)(2,1)}), bf16[1024,1536]{1,0:T(8,128)(2,1)}) %all-gather.8.cloned.1.call-update) | async-done | bytes 3145744 | tf_op jit(solution)/shard_map/all_gather | solution.py:60
  438.9 6.8 fusion.5
  445.7 4.6 fusion.71
  450.4 8.1 convolution_multiply_fusion
  458.5 2.4 copy.21
  460.9 4.3 convolution_multiply_fusion.1
  465.5 49.5 %reduce-scatter.4.cloned.1.call-done = f32[256,1536]{1,0:T(8,128)} async-done(((f32[1024,1536]{1,0:T(8,128)}), f32[256,1536]{1,0:T(8,128)}) %reduce-scatter.4.cloned.1.call-update) | async-done | bytes 1572880 | tf_op jit(solution)/shard_map/reduce_scatter | solution.py:91
  516.8 3.9 multiply_reduce_fusion.49
  520.8 18.9 %multiply_reduce_fusion = (f32[1536]{0:T(1024)S(1)}, f32[1536]{0:T(1024)S(1)}, f32[1536]{0:T(1024)S(1)}, f32[1536]{0:T(1024)S(1)}, f32[1536]{0:T(1024)S(1)}, /*i...) fusion(f32[2,10,38,1536]{3,0,2,1:T(2,128)} %copy-done, ...), kind=kLoop, calls=%fused_computation.127 | loop fusion | flops 16880640 | bytes 33150976 | tf_op jit(solution)/shard_map/reduce_sum | solution.py:112
  540.0 13.1 %multiply_reduce_fusion.18 = (f32[1536]{0:T(1024)S(1)}, f32[1536]{0:T(1024)S(1)}, f32[1536]{0:T(1024)S(1)}, f32[1536]{0:T(1024)S(1)}, f32[1536]{0:T(1024)S(1)}, ...) fusion(f32[2,4,32,1536]{3,0,2,1:T(2,128)S(1)} %get-tuple-elemen, ...), kind=kLoop, calls=%fused_computation.145 | loop fusion | flops 14128128 | bytes 29995008 | tf_op jit(solution)/shard_map/reduce_sum | solution.py:112
  553.1 9.1 multiply_reduce_fusion.36
  564.7 2.3 collective-permute-start.4
  569.0 94.1 %collective-permute-done.4 = f32[2,3,32,1536]{3,0,2,1:T(2,128)S(1)} collective-permute-done((f32[2,3,32,1536]{3,0,2,1:T(2,128)}, f32[2,3,32,1536]{3,0,2,1:T(2,128)S(1)}, u32[]{:S(2)}, u32[]{:S(2)}) %collective-permute-start.4) | collective-permute-done | bytes 1179680 | tf_op jit(solution)/shard_map/ppermute | solution.py:14
  665.2 4.7 collective-permute-start.6
  669.9 4.0 collective-permute-start.7
  675.1 11.8 %collective-permute-done.6 = f32[2,10,3,1536]{3,0,2,1:T(2,128)S(1)} collective-permute-done((f32[2,10,3,1536]{3,0,2,1:T(2,128)}, f32[2,10,3,1536]{3,0,2,1:T(2,128)S(1)}, u32[]{:S(2)}, u32[]{:S(2)}) %collective-permute-start.6) | collective-permute-done | bytes 368672 | tf_op jit(solution)/shard_map/ppermute | solution.py:15
  686.9 6.2 pad_maximum_fusion
  693.6 40.7 %fusion.23 = bf16[2,4,32,1536]{3,0,2,1:T(2,128)(2,1)S(1)} fusion(f32[2,10,35,1536]{3,0,2,1:T(2,128)S(1)} %get-tuple-element.114, f32[2,4,32,1536]{3,0,2,1:T(2,128)S(1)} %get-tuple-element.110, f32[2,3,32,1536]{3,0,2,1:T(2,128)S(1)} %collective-permute-done.4, f32[2,10,35,1536]{3,0,2,1:T(2,128)S(1)} %get-tuple-element.113, ...), kind=kLoop, calls=%fused_computation.40 | loop fusion | flops 41287680 | bytes 72652800 | tf_op jit(solution)/shard_map/convert_element_type | solution.py:131
  735.3 127.0 %reduce-scatter.6.cloned.1.call-done = f32[48,768]{1,0:T(8,128)} async-done(((f32[1536,768]{1,0:T(8,128)}), f32[48,768]{1,0:T(8,128)}) %reduce-scatter.6.cloned.1.call-update) | async-done | bytes 147472 | tf_op jit(solution)/shard_map/reduce_scatter | solution.py:82
  862.2 169.4 %all-reduce.2.cloned.1.call-done = f32[7,7,1536]{2,1,0:T(8,128)} async-done(((f32[7,7,1536]{2,1,0:T(8,128)}), f32[7,7,1536]{2,1,0:T(8,128)}) %all-reduce.2.cloned.1.call-update) | async-done | bytes 301072 | tf_op jit(solution)/shard_map/psum | solution.py:119
  (303 shorter events, 31.1 us)
Async XLA Ops:
  7.2 121.2 %all-gather.6.cloned.1.call-start = ((), (), s32[]{:S(2)}) async-start(), calls=%async_computation.3 | async-start | bytes 3932160 | tf_op jit(solution)/shard_map/all_gather | solution.py:29
  7.9 185.5 %all-gather.14.cloned.1.call-start = ((), (), s32[]{:S(2)}) async-start(), calls=%async_computation.7 | async-start | bytes 2433024 | tf_op jit(solution)/shard_map/all_gather | solution.py:62
  9.0 36.2 %collective-permute-start = (bf16[2,3,32,1536]{3,0,2,1:T(2,128)(2,1)S(1)}, bf16[2,3,32,1536]{3,0,2,1:T(2,128)(2,1)S(1)}, u32[]{:S(2)}, u32[]{:S(2)}) collective-permute-start(bf16[2,3,32,1536]{3,0,2,1:T(2,128)(2,1)S(1)} %copy.37), channel_id=1, source_target_pairs={{0,4},{4,8},{8,12},{12,16},{16,20},{20,24},{24,28},{28,32},{32,36}... | collective-permute-start | bytes 1769480 | tf_op jit(solution)/shard_map/ppermute | solution.py:14
  14.1 32.5 %collective-permute-start.1 = (bf16[2,3,32,1536]{3,0,2,1:T(2,128)(2,1)S(1)}, bf16[2,3,32,1536]{3,0,2,1:T(2,128)(2,1)S(1)}, u32[]{:S(2)}, u32[]{:S(2)}) collective-permute-start(bf16[2,3,32,1536]{3,0,2,1:T(2,128)(2,1)S(1)} %copy.38), channel_id=1, source_target_pairs={{4,0},{8,4},{12,8},{16,12},{20,16},{24,20},{28,24},{32,28},{36,32}... | collective-permute-start | bytes 1769480 | tf_op jit(solution)/shard_map/ppermute | solution.py:15
  15.4 235.3 %all-gather.12.cloned.1.call-start = ((), (), s32[]{:S(2)}) async-start(), calls=%async_computation.6 | async-start | bytes 3932160 | tf_op jit(solution)/shard_map/all_gather | solution.py:61
  47.3 12.9 %collective-permute-start.2 = (bf16[2,10,3,1536]{3,0,2,1:T(2,128)(2,1)S(1)}, bf16[2,10,3,1536]{3,0,2,1:T(2,128)(2,1)S(1)}, u32[]{:S(2)}, u32[]{:S(2)}) collective-permute-start(bf16[2,10,3,1536]{3,0,2,1:T(2,128)(2,1)S(1)} %get-tuple-element.117), channel_id=1, source_target_pairs={{0,1},{1,2},{2,3},{4,5},{5,6},{6,7},{8,9},{9,10},{10,11},{12,13},{... | collective-permute-start | bytes 552968 | tf_op jit(solution)/shard_map/ppermute | solution.py:14
  55.9 8.4 collective-permute-start.3
  67.2 55.9 %copy-start = (f32[2,10,38,1536]{3,0,2,1:T(2,128)}, f32[2,10,38,1536]{3,0,2,1:T(2,128)S(1)}, u32[]{:S(2)}) copy-start(f32[2,10,38,1536]{3,0,2,1:T(2,128)S(1)} %maximum_convert_fusion) | copy-start | bytes 14008324
  127.7 255.2 %all-gather.10.cloned.1.call-start = ((), (), s32[]{:S(2)}) async-start(), calls=%async_computation.5 | async-start | bytes 2433024 | tf_op jit(solution)/shard_map/all_gather | solution.py:68
  128.3 310.6 %all-gather.8.cloned.1.call-start = ((), (), s32[]{:S(2)}) async-start(), calls=%async_computation.4 | async-start | bytes 3932160 | tf_op jit(solution)/shard_map/all_gather | solution.py:60
  135.6 379.4 %reduce-scatter.4.cloned.1.call-start = ((), (), s32[]{:S(2)}) async-start(), calls=%async_computation.8 | async-start | bytes 7864320 | tf_op jit(solution)/shard_map/reduce_scatter | solution.py:91
  450.3 285.0 %reduce-scatter.8.cloned.1.call-start = ((), (), s32[]{:S(2)}) async-start(), calls=%async_computation.10 | async-start | bytes 4866048 | tf_op jit(solution)/shard_map/reduce_scatter | solution.py:81
  458.5 403.8 %reduce-scatter.6.cloned.1.call-start = ((), (), s32[]{:S(2)}) async-start(), calls=%async_computation.9 | async-start | bytes 4866048 | tf_op jit(solution)/shard_map/reduce_scatter | solution.py:82
  465.3 51.5 %copy-start.2 = (f32[2,4,32,1536]{3,0,2,1:T(2,128)S(1)}, f32[2,4,32,1536]{3,0,2,1:T(2,128)}, u32[]{:S(2)}) copy-start(f32[2,4,32,1536]{3,0,2,1:T(2,128)} %get-tuple-element.112) | copy-start | bytes 4718596
  465.3 566.3 %all-reduce.2.cloned.1.call-start = ((), (), s32[]{:S(2)}) async-start(), calls=%async_computation.11 | async-start | bytes 688128 | tf_op jit(solution)/shard_map/psum | solution.py:119
  520.7 19.2 %slice-start = ((s8[4669440]{0:T(1024)(128)(4,1)}), s8[4194304]{0:T(1024)(128)(4,1)S(1)}, s32[]{:S(2)}) async-start(s8[4669440]{0:T(1024)(128)(4,1)} %bitcast.34), calls=%async_computation.12 | async-start | bytes 8388608
  520.8 19.2 %slice-start.1 = ((s8[4669440]{0:T(1024)(128)(4,1)}), s8[475136]{0:T(1024)(128)(4,1)S(1)}, s32[]{:S(2)}) async-start(s8[4669440]{0:T(1024)(128)(4,1)} %bitcast.34), calls=%async_computation.13 | async-start | bytes 950272
  564.7 98.3 %collective-permute-start.4 = (f32[2,3,32,1536]{3,0,2,1:T(2,128)}, f32[2,3,32,1536]{3,0,2,1:T(2,128)S(1)}, u32[]{:S(2)}, u32[]{:S(2)}) collective-permute-start(f32[2,3,32,1536]{3,0,2,1:T(2,128)} %get-tuple-element.119), channel_id=1, source_target_pairs={{0,4},{4,8},{8,12},{12,16},{16,20},{20,24},{24,28},{28,32},{32,36}... | collective-permute-start | bytes 3538952 | tf_op jit(solution)/shard_map/ppermute | solution.py:14
  567.1 96.0 %collective-permute-start.5 = (f32[2,3,32,1536]{3,0,2,1:T(2,128)}, f32[2,3,32,1536]{3,0,2,1:T(2,128)}, u32[]{:S(2)}, u32[]{:S(2)}) collective-permute-start(f32[2,3,32,1536]{3,0,2,1:T(2,128)} %get-tuple-element.120), channel_id=1, source_target_pairs={{4,0},{8,4},{12,8},{16,12},{20,16},{24,20},{28,24},{32,28},{36,32}... | collective-permute-start | bytes 3538952 | tf_op jit(solution)/shard_map/ppermute | solution.py:15
  665.2 21.7 %collective-permute-start.6 = (f32[2,10,3,1536]{3,0,2,1:T(2,128)}, f32[2,10,3,1536]{3,0,2,1:T(2,128)S(1)}, u32[]{:S(2)}, u32[]{:S(2)}) collective-permute-start(f32[2,10,3,1536]{3,0,2,1:T(2,128)} %get-tuple-element.115), channel_id=1, source_target_pairs={{1,0},{2,1},{3,2},{5,4},{6,5},{7,6},{9,8},{10,9},{11,10},{13,12},{... | collective-permute-start | bytes 1105928 | tf_op jit(solution)/shard_map/ppermute | solution.py:15
  669.9 17.0 %collective-permute-start.7 = (f32[2,10,3,1536]{3,0,2,1:T(2,128)}, f32[2,10,3,1536]{3,0,2,1:T(2,128)S(1)}, u32[]{:S(2)}, u32[]{:S(2)}) collective-permute-start(f32[2,10,3,1536]{3,0,2,1:T(2,128)} %get-tuple-element.116), channel_id=1, source_target_pairs={{0,1},{1,2},{2,3},{4,5},{5,6},{6,7},{8,9},{9,10},{10,11},{12,13},{... | collective-permute-start | bytes 1105928 | tf_op jit(solution)/shard_map/ppermute | solution.py:14
  674.7 18.5 %copy-start.4 = (f32[2,2,2,16,2,1536]{5,0,4,3,2,1:T(2,128)S(1)}, f32[2,2,2,16,2,1536]{5,0,4,3,2,1:T(2,128)}, u32[]{:S(2)}) copy-start(f32[2,2,2,16,2,1536]{5,0,4,3,2,1:T(2,128)} %copy.21) | copy-start | bytes 4718596
  674.7 18.5 %copy-start.9 = (f32[1536]{0:T(1024)S(1)}, f32[1536]{0:T(1024)}, u32[]{:S(2)}) copy-start(f32[1536]{0:T(1024)} %get-tuple-element.69) | copy-start | bytes 18436
  674.7 18.5 %copy-start.11 = (f32[1536]{0:T(1024)S(1)}, f32[1536]{0:T(1024)}, u32[]{:S(2)}) copy-start(f32[1536]{0:T(1024)} %get-tuple-element.70) | copy-start | bytes 18436
  674.7 18.5 %copy-start.13 = (f32[1536]{0:T(1024)S(1)}, f32[1536]{0:T(1024)}, u32[]{:S(2)}) copy-start(f32[1536]{0:T(1024)} %get-tuple-element.71) | copy-start | bytes 18436
  674.7 18.5 %copy-start.15 = (f32[1536]{0:T(1024)S(1)}, f32[1536]{0:T(1024)}, u32[]{:S(2)}) copy-start(f32[1536]{0:T(1024)} %get-tuple-element.72) | copy-start | bytes 18436
  674.7 18.5 %copy-start.17 = (f32[1536]{0:T(1024)S(1)}, f32[1536]{0:T(1024)}, u32[]{:S(2)}) copy-start(f32[1536]{0:T(1024)} %get-tuple-element.73) | copy-start | bytes 18436
  674.7 18.5 %copy-start.19 = (f32[1536]{0:T(1024)S(1)}, f32[1536]{0:T(1024)}, u32[]{:S(2)}) copy-start(f32[1536]{0:T(1024)} %get-tuple-element.74) | copy-start | bytes 18436
  674.8 18.5 %copy-start.21 = (f32[1536]{0:T(1024)S(1)}, f32[1536]{0:T(1024)}, u32[]{:S(2)}) copy-start(f32[1536]{0:T(1024)} %get-tuple-element.75) | copy-start | bytes 18436
  674.8 18.5 %copy-start.23 = (f32[1536]{0:T(1024)S(1)}, f32[1536]{0:T(1024)}, u32[]{:S(2)}) copy-start(f32[1536]{0:T(1024)} %get-tuple-element.76) | copy-start | bytes 18436
  674.8 18.5 %copy-start.25 = (f32[1536]{0:T(1024)S(1)}, f32[1536]{0:T(1024)}, u32[]{:S(2)}) copy-start(f32[1536]{0:T(1024)} %get-tuple-element.77) | copy-start | bytes 18436
  674.8 18.5 %copy-start.27 = (f32[1536]{0:T(1024)S(1)}, f32[1536]{0:T(1024)}, u32[]{:S(2)}) copy-start(f32[1536]{0:T(1024)} %get-tuple-element.78) | copy-start | bytes 18436
  (77 other events, 862.2 us)
Sparse Core Ops, SparseCore 0:
  9.7 52.0 all-gather.5
  63.4 129.9 all-gather.13
  195.6 54.9 all-gather.11
  252.2 130.6 all-gather.9
  384.4 54.4 all-gather.7
  450.4 64.5 reduce-scatter.3
  518.0 174.4 reduce-scatter.7
  695.5 166.7 reduce-scatter.5
  867.6 163.9 all-reduce.1
where the time goes:
time: 1040 us
  waiting for transfers between devices  782 us (75%)
  other arithmetic  161 us (15%)
  matrix products  30.7 us (3%)
  starting transfers between devices  29.9 us (3%)
  local copies, waits for them, and re-layouts  20.9 us (2%)
  between operations  16.1 us (2%)
    psum x1, waiting for transfers between devices, local(): grad_kernel = lax.psum(kernel_local, ('rows', 'cols'))  169 us
    reduce_scatter x1, waiting for transfers between devices, local(): lax.psum_scatter(lax.dot_general(normed_all, hidden_grad, (((0,), (0,)),...  127 us
    all_gather x1, waiting for transfers between devices, local(): lax.all_gather(w_out, 'rows', axis=1, tiled=True)  125 us
    ppermute x4, waiting for transfers between devices, with_halo(): before = lax.ppermute(last, axis, up)  123 us
    all_gather x1, waiting for transfers between devices, local(): normed_all = lax.all_gather(norm_output, 'cols', axis=0, tiled=True)  57.3 us
    all_gather x1, waiting for transfers between devices, local(): w_in_cols = lax.all_gather(w_in, 'rows', axis=0, tiled=True)  57.2 us
    all_gather x1, waiting for transfers between devices, local(): branch_all = lax.all_gather(branch_grad, 'cols', axis=0, tiled=True)  56 us
    reduce_sum x1, other arithmetic, local(): mean_val = jnp.mean(conv_out, axis=-1, keepdims=True)  55.5 us
  transfers between devices with their start and end apart: 17, of which 11 were waited for; matrix products, arithmetic and copies ran while one was open for 19% of the time, Pallas kernels for 0%

commit v1 on v0

--- a/solution.py
+++ b/solution.py
@@ -17,18 +17,68 @@
     return value
 
 
+def swap_with(value, axis, bit):
+    peers = lax.axis_size(axis)
+    return lax.ppermute(value, axis, [(i, i ^ (1 << bit)) for i in range(peers)])
+
+
+def gather_rows(value, axis, order):
+    me = lax.axis_index(axis)
+    for bit in order:
+        other = swap_with(value, axis, bit)
+        b = (me >> bit) & 1
+        both = jnp.concatenate([value, other, value], axis=0)
+        value = lax.dynamic_slice_in_dim(both, b * value.shape[0], 2 * value.shape[0], axis=0)
+    n = len(order)
+    block = value.shape[0] >> n
+    rest = value.shape[1:]
+    value = value.reshape((2,) * n + (block,) + rest)
+    perm = [n - 1 - order.index(k) for k in reversed(range(n))]
+    value = value.transpose(perm + list(range(n, value.ndim)))
+    return value.reshape((block << n,) + rest)
+
+
+def scatter_rows(value, axis, order):
+    me = lax.axis_index(axis)
+    n = len(order)
+    block = value.shape[0] >> n
+    rest = value.shape[1:]
+    value = value.reshape((2,) * n + (block,) + rest)
+    perm = [n - 1 - order[j] for j in range(n)]
+    value = value.transpose(perm + list(range(n, value.ndim))).reshape((block << n,) + rest)
+    for bit in order:
+        half = value.shape[0] // 2
+        b = (me >> bit) & 1
+        keep = lax.dynamic_slice_in_dim(value, b * half, half, axis=0)
+        send = lax.dynamic_slice_in_dim(value, (1 - b) * half, half, axis=0)
+        value = keep + swap_with(send, axis, bit)
+    return value
+
+
 def local(block_input, token_grads, conv_kernel, layer_norm_gain, w_in, w_out, layer_scale):
     images, tile_rows, tile_cols, channel_total = block_input.shape
     kernel_size = conv_kernel.shape[0]
     kernel_reach = kernel_size // 2
     n_rows = lax.axis_size("rows")
     n_cols = lax.axis_size("cols")
+    row_bits = n_rows.bit_length() - 1
+    col_bits = n_cols.bit_length() - 1
     run_count = tile_rows // 2
     half_cols = tile_cols // 2
     col_index = lax.axis_index("cols")
-    group_rows = lax.all_gather(token_grads, "cols", axis=1, tiled=True)
-    group_rows = group_rows.reshape(images, run_count, n_cols, half_cols, 4 * channel_total)
-    merged = lax.dynamic_index_in_dim(group_rows, col_index, 2, keepdims=False)
+
+    w_in_cols = gather_rows(w_in, "rows", (4, 2, 3, 1, 0))
+    w_out_cols_t = gather_rows(w_out.T, "rows", (4, 2, 3, 0, 1))
+
+    tokens = token_grads.reshape(images, 2, half_cols, 4 * channel_total)
+    first_half = col_index // 2
+    send_a = lax.dynamic_index_in_dim(tokens, first_half, 1, keepdims=False)
+    send_b = lax.dynamic_index_in_dim(tokens, 1 - first_half, 1, keepdims=False)
+    got_a = lax.ppermute(send_a, "cols", [(s, 2 * (s % 2) + s // 2) for s in range(n_cols)])
+    got_b = lax.ppermute(send_b, "cols", [(s, 2 * (s % 2) + 1 - s // 2) for s in range(n_cols)])
+    merged = lax.dynamic_slice_in_dim(
+        jnp.stack([got_a, got_b, got_a], axis=1), col_index % 2, 2, axis=1
+    )
     out_grad = merged.reshape(images, run_count, half_cols, 2, 2, channel_total)
     out_grad = out_grad.transpose(0, 1, 3, 2, 4, 5).reshape(
         images, tile_rows, tile_cols, channel_total
@@ -59,35 +109,21 @@
     )
     branch_all = lax.all_gather(branch_grad, "cols", axis=0, tiled=True)
     normed_all = lax.all_gather(norm_output, "cols", axis=0, tiled=True)
-    w_in_cols = lax.all_gather(w_in, "rows", axis=0, tiled=True)
     pre = jnp.dot(normed_all, w_in_cols, preferred_element_type=jnp.float32)
     cdf = 0.5 * (1.0 + lax.erf(pre * 0.7071067811865476))
     hidden = (pre * cdf).astype(jnp.bfloat16)
-    back_hidden = lax.dot_general(
-        branch_all,
-        lax.all_gather(w_out, "rows", axis=1, tiled=True),
-        (((1,), (1,)), ((), ())),
-        preferred_element_type=jnp.float32,
-    )
+    back_hidden = jnp.dot(branch_all, w_out_cols_t, preferred_element_type=jnp.float32)
     density = jnp.exp(-0.5 * pre * pre) * 0.3989422804014327
     hidden_grad = (back_hidden * (cdf + pre * density)).astype(jnp.bfloat16)
     scale = 1.0 / float(images * tile_rows * tile_cols * n_rows * n_cols) ** 0.5
-    out_terms = (
-        lax.dot_general(
-            hidden, branch_all, (((0,), (0,)), ((), ())), preferred_element_type=jnp.float32
-        )
-        * scale
+    out_terms_t = lax.dot_general(
+        branch_all, hidden, (((0,), (0,)), ((), ())), preferred_element_type=jnp.float32
     )
-    grad_w2 = lax.psum_scatter(out_terms, "rows", scatter_dimension=1, tiled=True)
-    grad_w1 = lax.psum_scatter(
-        lax.dot_general(
-            normed_all, hidden_grad, (((0,), (0,)), ((), ())), preferred_element_type=jnp.float32
-        )
-        * scale,
-        "rows",
-        scatter_dimension=0,
-        tiled=True,
+    in_terms = lax.dot_general(
+        normed_all, hidden_grad, (((0,), (0,)), ((), ())), preferred_element_type=jnp.float32
     )
+    grad_w1 = scatter_rows(in_terms, "rows", (0, 1, 3, 2, 4)) * scale
+    grad_w2 = (scatter_rows(out_terms_t, "rows", (1, 0, 3, 2, 4)) * scale).T
     normed_grad = lax.psum_scatter(
         lax.dot_general(
             hidden_grad, w_in_cols, (((1,), (1,)), ((), ())), preferred_element_type=jnp.float32
@@ -115,8 +151,12 @@
                 )
             )
         kernel_rows.append(jnp.stack(row_terms))
-    kernel_local = jnp.stack(kernel_rows) * scale
-    grad_kernel = lax.psum(kernel_local, ("rows", "cols"))
+    grad_kernel = jnp.stack(kernel_rows)
+    for bit in range(col_bits):
+        grad_kernel = grad_kernel + swap_with(grad_kernel, "cols", bit)
+    for bit in (0, 1, 3, 2, 4)[:row_bits]:
+        grad_kernel = grad_kernel + swap_with(grad_kernel, "rows", bit)
+    grad_kernel = grad_kernel * scale
     grad_pad = with_halo(convolution_gradient, (("rows", 1), ("cols", 2)), kernel_reach)
     total = out_grad.astype(jnp.float32)
     for r in range(kernel_size):

time: 1040 us -> 612 us (0.59)
  waiting for transfers between devices: 782 us -> 261 us
  starting transfers between devices: 29.9 us -> 79.6 us
  other arithmetic: 161 us -> 186 us
  local copies, waits for them, and re-layouts: 20.9 us -> 37.8 us
    ppermute x0 -> x29, waiting for transfers between devices: none -> 234 us  [the longest x27 224 us: swap_with(): return lax.ppermute(value, axis, [(i, i ^ 1 << bit) for i in range(peers)])]
    all_gather x3 -> x0, waiting for transfers between devices: 183 us -> none  [the longest x1 125 us: local(): lax.all_gather(w_out, 'rows', axis=1, tiled=True)]
    psum x1 -> x0, waiting for transfers between devices: 169 us -> none  [local(): grad_kernel = lax.psum(kernel_local, ('rows', 'cols'))]
    reduce_scatter x2 -> x0, waiting for transfers between devices: 127 us -> none  [the longest x1 127 us: local(): lax.psum_scatter(lax.dot_general(normed_all, hidden_grad, (((0,), (0,)),...]
    ppermute x4, waiting for transfers between devices: 123 us -> 22.2 us  [with_halo(): before = lax.ppermute(last, axis, up)]
    all_gather x1, waiting for transfers between devices: 57.3 us -> 0.01 us  [local(): normed_all = lax.all_gather(norm_output, 'cols', axis=0, tiled=True)]
    all_gather x1, waiting for transfers between devices: 56 us -> 0.01 us  [local(): branch_all = lax.all_gather(branch_grad, 'cols', axis=0, tiled=True)]
    ppermute x0 -> x29, starting transfers between devices: none -> 54.6 us  [the longest x27 52.3 us: swap_with(): return lax.ppermute(value, axis, [(i, i ^ 1 << bit) for i in range(peers)])]
  transfers between devices with their start and end apart: 17 -> 40, of which waited for: 11 -> 20; matrix products, arithmetic and copies ran while one was open for 19% -> 27% of each run, Pallas kernels for 0% -> 0%
where the time goes in v1:
time: 612 us; the launch traced here: 607 us
  waiting for transfers between devices  261 us (43%)
  other arithmetic  186 us (30%)
  starting transfers between devices  79.6 us (13%)
  local copies, waits for them, and re-layouts  37.8 us (6%)
  matrix products  26.7 us (4%)
  between operations  16.5 us (3%)
    ppermute x27, waiting for transfers between devices, swap_with(): return lax.ppermute(value, axis, [(i, i ^ 1 << bit) for i in range(peers)])  224 us
    reduce_sum x1, other arithmetic, local(): mean_val = jnp.mean(conv_out, axis=-1, keepdims=True)  56.1 us
    ppermute x27, starting transfers between devices, swap_with(): return lax.ppermute(value, axis, [(i, i ^ 1 << bit) for i in range(peers)])  52.3 us
    reduce_sum x3, other arithmetic, local(): jnp.sum(convolution_gradient * padded[:, r:r + tile_rows, s:s + tile_cols...  42.3 us
    convert_element_type x1, other arithmetic, local(): input_grad = total.astype(jnp.bfloat16)  38.7 us
    ppermute x4, waiting for transfers between devices, with_halo(): before = lax.ppermute(last, axis, up)  22.2 us
    concatenate x10, other arithmetic, gather_rows(): both = jnp.concatenate([value, other, value], axis=0)  17.3 us
    ppermute x4, starting transfers between devices, with_halo(): before = lax.ppermute(last, axis, up)  16.6 us
  transfers between devices with their start and end apart: 40, of which 20 were waited for; matrix products, arithmetic and copies ran while one was open for 27% of the time, Pallas kernels for 0%

profile of v1, /device:TPU:1, one launch (start us, length us, event | category | flops | bytes accessed | tf_op | source)
XLA Modules:
  0.0 607.3 jit_solution(6501913082351932144)
XLA Ops:
  9.2 4.5 collective-permute-start.2
  16.1 22.2 %collective-permute-done.2 = bf16[2,3,32,1536]{3,0,2,1:T(2,128)(2,1)S(1)} collective-permute-done((bf16[2,3,32,1536]{3,0,2,1:T(2,128)(2,1)S(1)}, bf16[2,3,32,1536]{3,0,2,1:T(2,128)(2,1)S(1)}, u32[]{:S(2)}, u32[]{:S(2)}) %collective-permute-start.2) | collective-permute-done | bytes 589856 | tf_op jit(solution)/shard_map/ppermute | solution.py:14
  40.4 6.6 %collective-permute-start.4 = (bf16[2,10,3,1536]{3,0,2,1:T(2,128)(2,1)S(1)}, bf16[2,10,3,1536]{3,0,2,1:T(2,128)(2,1)S(1)}, u32[]{:S(2)}, u32[]{:S(2)}) collective-permute-start(bf16[2,10,3,1536]{3,0,2,1:T(2,128)(2,1)S(1)} %get-tuple-element.117), channel_id=1, source_target_pairs={{0,1},{1,2},{2,3},{4,5},{5,6},{6,7},{8,9},{9,10},{10,11},{12,13},{... | collective-permute-start | bytes 552968 | tf_op jit(solution)/shard_map/ppermute | solution.py:14
  50.4 5.0 collective-permute-done.5
  58.7 56.1 %fusion.90 = (f32[2,4,32]{0,2,1:T(8,128)S(1)}, f32[2,4,32,1536]{3,0,2,1:T(2,128)}) fusion(f32[2,10,38,1536]{3,0,2,1:T(2,128)S(1)} %maximum_convert_fusion, f32[1536]{0:T(1024)S(1)} %get-tuple-element.108, f32[1536]{0:T(1024)S(1)} %get-tuple-element.109, f32[1536]{0:T(1024)S(1)} %get-tuple-element.62, f32[1536]{0:T(1024)S(1)} %get-tuple-element.63, ...), kind=kLoop, calls=%fused_computation.328 | loop fusion | flops 38534912 | bytes 78945280 | tf_op jit(solution)/shard_map/reduce_sum | solution.py:94
  122.1 8.4 %collective-permute-done = bf16[2,16,6144]{2,1,0:T(8,128)(2,1)S(1)} collective-permute-done((bf16[2,16,6144]{2,1,0:T(8,128)(2,1)S(1)}, bf16[2,16,6144]{2,1,0:T(8,128)(2,1)S(1)}, u32[]{:S(2)}, u32[]{:S(2)}) %collective-permute-start) | collective-permute-done | bytes 393248 | tf_op jit(solution)/shard_map/ppermute | solution.py:77
  138.5 10.6 %collective-permute-start.11 = (bf16[48,768]{1,0:T(8,128)(2,1)S(1)}, bf16[48,768]{1,0:T(8,128)(2,1)S(1)}, u32[]{:S(2)}, u32[]{:S(2)}) collective-permute-start(bf16[48,768]{1,0:T(8,128)(2,1)S(1)} %copy-done.95), channel_id=1, source_target_pairs={{0,64},{4,68},{8,72},{12,76},{16,80},{20,84},{24,88},{28,92},{32,9... | collective-permute-start | bytes 221192 | tf_op jit(solution)/shard_map/ppermute | solution.py:22
  159.3 6.1 %collective-permute-done.7 = bf16[96,768]{1,0:T(8,128)(2,1)S(1)} collective-permute-done((bf16[96,768]{1,0:T(8,128)(2,1)S(1)}, bf16[96,768]{1,0:T(8,128)(2,1)S(1)}, u32[]{:S(2)}, u32[]{:S(2)}) %collective-permute-start.7) | collective-permute-done | bytes 147488 | tf_op jit(solution)/shard_map/ppermute | solution.py:22
  167.8 6.5 %collective-permute-done.8 = bf16[192,768]{1,0:T(8,128)(2,1)S(1)} collective-permute-done((bf16[192,768]{1,0:T(8,128)(2,1)S(1)}, bf16[192,768]{1,0:T(8,128)(2,1)S(1)}, u32[]{:S(2)}, u32[]{:S(2)}) %collective-permute-start.8) | collective-permute-done | bytes 294944 | tf_op jit(solution)/shard_map/ppermute | solution.py:22
  179.3 15.1 %collective-permute-done.9 = bf16[384,768]{1,0:T(8,128)(2,1)} collective-permute-done((bf16[384,768]{1,0:T(8,128)(2,1)S(1)}, bf16[384,768]{1,0:T(8,128)(2,1)}, u32[]{:S(2)}, u32[]{:S(2)}) %collective-permute-start.9) | collective-permute-done | bytes 589856 | tf_op jit(solution)/shard_map/ppermute | solution.py:22
  199.3 20.4 %collective-permute-done.15 = bf16[768,768]{1,0:T(8,128)(2,1)} collective-permute-done((bf16[768,768]{1,0:T(8,128)(2,1)S(1)}, bf16[768,768]{1,0:T(8,128)(2,1)}, u32[]{:S(2)}, u32[]{:S(2)}) %collective-permute-start.15) | collective-permute-done | bytes 1179680 | tf_op jit(solution)/shard_map/ppermute | solution.py:22
  219.7 4.6 fusion.7
  226.0 3.8 fusion.9
  231.4 6.9 %fusion.94 = f32[1024,768]{1,0:T(8,128)} fusion(bf16[1024,1536]{1,0:T(8,128)(2,1)} %all-gather.5.cloned.1.call-done, bf16[1536,768]{1,0:T(8,128)(2,1)} %bitcast.71), kind=kOutput, calls=%fused_computation.332 | convolution fusion | flops 2415919104 | bytes 8650752 | tf_op jit(solution)/shard_map/dot_general | solution.py:112
  238.3 6.8 %fusion.5 = bf16[1024,768]{1,0:T(8,128)(2,1)S(1)} fusion(f32[1024,768]{1,0:T(8,128)} %fusion.94, bf16[1024,1536]{1,0:T(8,128)(2,1)} %all-gather.3.cloned.1.call-done, bf16[1536,768]{1,0:T(8,128)(2,1)} %bitcast.73), kind=kOutput, calls=%fused_computation.14 | convolution fusion | flops 2423783424 | bytes 10223616 | tf_op jit(solution)/shard_map/dot_general | solution.py:115
  245.1 4.8 fusion.95
  249.9 5.6 fusion.26
  267.4 39.7 %collective-permute-done.25 = f32[768,768]{1,0:T(8,128)} collective-permute-done((f32[768,768]{1,0:T(8,128)}, f32[768,768]{1,0:T(8,128)}, u32[]{:S(2)}, u32[]{:S(2)}) %collective-permute-start.25) | collective-permute-done | bytes 2359328 | tf_op jit(solution)/shard_map/ppermute | solution.py:22
  312.6 38.3 %collective-permute-done.20 = f32[768,768]{1,0:T(8,128)} collective-permute-done((f32[768,768]{1,0:T(8,128)}, f32[768,768]{1,0:T(8,128)}, u32[]{:S(2)}, u32[]{:S(2)}) %collective-permute-start.20) | collective-permute-done | bytes 2359328 | tf_op jit(solution)/shard_map/ppermute | solution.py:22
  355.2 21.0 %collective-permute-done.26 = f32[384,768]{1,0:T(8,128)} collective-permute-done((f32[384,768]{1,0:T(8,128)}, f32[384,768]{1,0:T(8,128)}, u32[]{:S(2)}, u32[]{:S(2)}) %collective-permute-start.26) | collective-permute-done | bytes 1179680 | tf_op jit(solution)/shard_map/ppermute | solution.py:22
  386.2 4.8 collective-permute-done.27
  392.9 4.2 multiply_reduce_fusion.49
  397.5 20.1 %multiply_reduce_fusion = (f32[1536]{0:T(1024)S(1)}, f32[1536]{0:T(1024)S(1)}, f32[1536]{0:T(1024)S(1)}, f32[1536]{0:T(1024)S(1)}, f32[1536]{0:T(1024)S(1)}, /*i...) fusion(f32[2,10,38,1536]{3,0,2,1:T(2,128)} %copy-done, ...), kind=kLoop, calls=%fused_computation.144 | loop fusion | flops 16880640 | bytes 33150976 | tf_op jit(solution)/shard_map/reduce_sum | solution.py:148
  417.6 13.1 %multiply_reduce_fusion.18 = (f32[1536]{0:T(1024)S(1)}, f32[1536]{0:T(1024)S(1)}, f32[1536]{0:T(1024)S(1)}, f32[1536]{0:T(1024)S(1)}, f32[1536]{0:T(1024)S(1)}, ...) fusion(f32[2,4,32,1536]{3,0,2,1:T(2,128)S(1)} %get-tuple-elemen, ...), kind=kLoop, calls=%fused_computation.162 | loop fusion | flops 14128128 | bytes 29995008 | tf_op jit(solution)/shard_map/reduce_sum | solution.py:148
  430.7 9.1 %multiply_reduce_fusion.36 = (f32[1536]{0:T(1024)S(1)}, f32[1536]{0:T(1024)S(1)}, f32[1536]{0:T(1024)S(1)}, f32[1536]{0:T(1024)S(1)}, f32[1536]{0:T(1024)S(1)}, ...) fusion(f32[2,4,32,1536]{3,0,2,1:T(2,128)S(1)} %get-tuple-elemen, ...), kind=kLoop, calls=%fused_computation.180 | loop fusion | flops 10203648 | bytes 22099968 | tf_op jit(solution)/shard_map/reduce_sum | solution.py:148
  442.4 9.7 %collective-permute-start.30 = (f32[7,7,1536]{2,1,0:T(8,128)S(1)}, f32[7,7,1536]{2,1,0:T(8,128)S(1)}, u32[]{:S(2)}, u32[]{:S(2)}) collective-permute-start(f32[7,7,1536]{2,1,0:T(8,128)S(1)} %bitcast_dynamic-update-slice_fusion), channel_id=1, source_target_pairs={{0,1},{1,0},{2,3},{3,2},{4,5},{5,4},{6,7},{7,6},{8,9},{9,8},{10,11... | collective-permute-start | bytes 903176 | tf_op jit(solution)/shard_map/ppermute | solution.py:22
  456.1 5.9 collective-permute-start.28
  468.8 48.7 %collective-permute-done.31 = f32[7,7,1536]{2,1,0:T(8,128)S(1)} collective-permute-done((f32[7,7,1536]{2,1,0:T(8,128)S(1)}, f32[7,7,1536]{2,1,0:T(8,128)S(1)}, u32[]{:S(2)}, u32[]{:S(2)}) %collective-permute-start.31) | collective-permute-done | bytes 301088 | tf_op jit(solution)/shard_map/ppermute | solution.py:22
  517.7 5.7 collective-permute-start.29
  540.1 8.1 %collective-permute-done.34 = f32[7,7,1536]{2,1,0:T(8,128)S(1)} collective-permute-done((f32[7,7,1536]{2,1,0:T(8,128)S(1)}, f32[7,7,1536]{2,1,0:T(8,128)S(1)}, u32[]{:S(2)}, u32[]{:S(2)}) %collective-permute-start.34) | collective-permute-done | bytes 301088 | tf_op jit(solution)/shard_map/ppermute | solution.py:22
  551.1 4.8 pad_maximum_fusion
  560.0 38.7 %fusion.28 = bf16[2,4,32,1536]{3,0,2,1:T(2,128)(2,1)S(1)} fusion(f32[2,10,35,1536]{3,0,2,1:T(2,128)S(1)} %get-tuple-element.114, f32[2,4,32,1536]{3,0,2,1:T(2,128)S(1)} %get-tuple-element.110, f32[2,3,32,1536]{3,0,2,1:T(2,128)S(1)} %collective-permute-done.16, f32[2,10,35,1536]{3,0,2,1:T(2,128)S(1)} %get-tuple-element.113, ...), kind=kLoop, calls=%fused_computation.57 | loop fusion | flops 41287680 | bytes 72652800 | tf_op jit(solution)/shard_map/convert_element_type | solution.py:171
  (401 shorter events, 125.1 us)
Async XLA Ops:
  7.2 224.3 %all-gather.5.cloned.1.call-start = ((), (), s32[]{:S(2)}) async-start(), calls=%async_computation.2 | async-start | bytes 3932160 | tf_op jit(solution)/shard_map/all_gather | solution.py:111
  9.2 29.1 %collective-permute-start.2 = (bf16[2,3,32,1536]{3,0,2,1:T(2,128)(2,1)S(1)}, bf16[2,3,32,1536]{3,0,2,1:T(2,128)(2,1)S(1)}, u32[]{:S(2)}, u32[]{:S(2)}) collective-permute-start(bf16[2,3,32,1536]{3,0,2,1:T(2,128)(2,1)S(1)} %copy.45), channel_id=1, source_target_pairs={{0,4},{4,8},{8,12},{12,16},{16,20},{20,24},{24,28},{28,32},{32,36}... | collective-permute-start | bytes 1769480 | tf_op jit(solution)/shard_map/ppermute | solution.py:14
  14.3 25.3 %collective-permute-start.3 = (bf16[2,3,32,1536]{3,0,2,1:T(2,128)(2,1)S(1)}, bf16[2,3,32,1536]{3,0,2,1:T(2,128)(2,1)S(1)}, u32[]{:S(2)}, u32[]{:S(2)}) collective-permute-start(bf16[2,3,32,1536]{3,0,2,1:T(2,128)(2,1)S(1)} %copy.46), channel_id=1, source_target_pairs={{4,0},{8,4},{12,8},{16,12},{20,16},{24,20},{28,24},{32,28},{36,32}... | collective-permute-start | bytes 1769480 | tf_op jit(solution)/shard_map/ppermute | solution.py:15
  40.4 10.0 %collective-permute-start.4 = (bf16[2,10,3,1536]{3,0,2,1:T(2,128)(2,1)S(1)}, bf16[2,10,3,1536]{3,0,2,1:T(2,128)(2,1)S(1)}, u32[]{:S(2)}, u32[]{:S(2)}) collective-permute-start(bf16[2,10,3,1536]{3,0,2,1:T(2,128)(2,1)S(1)} %get-tuple-element.117), channel_id=1, source_target_pairs={{0,1},{1,2},{2,3},{4,5},{5,6},{6,7},{8,9},{9,10},{10,11},{12,13},{... | collective-permute-start | bytes 552968 | tf_op jit(solution)/shard_map/ppermute | solution.py:14
  119.4 118.9 %all-gather.3.cloned.1.call-start = ((), (), s32[]{:S(2)}) async-start(), calls=%async_computation.1 | async-start | bytes 3932160 | tf_op jit(solution)/shard_map/all_gather | solution.py:110
  119.8 10.6 %collective-permute-start = (bf16[2,16,6144]{2,1,0:T(8,128)(2,1)S(1)}, bf16[2,16,6144]{2,1,0:T(8,128)(2,1)S(1)}, u32[]{:S(2)}, u32[]{:S(2)}) collective-permute-start(bf16[2,16,6144]{2,1,0:T(8,128)(2,1)S(1)} %get-tuple-element.122), channel_id=1, source_target_pairs={{0,0},{1,2},{2,1},{3,3},{4,4},{5,6},{6,5},{7,7},{8,8},{9,10},{10,9... | collective-permute-start | bytes 1179656 | tf_op jit(solution)/shard_map/ppermute | solution.py:77
  121.8 10.1 %collective-permute-start.1 = (bf16[2,16,6144]{2,1,0:T(8,128)(2,1)S(1)}, bf16[2,16,6144]{2,1,0:T(8,128)(2,1)S(1)}, u32[]{:S(2)}, u32[]{:S(2)}) collective-permute-start(bf16[2,16,6144]{2,1,0:T(8,128)(2,1)S(1)} %get-tuple-element.121), channel_id=1, source_target_pairs={{0,1},{1,3},{2,0},{3,2},{4,5},{5,7},{6,4},{7,6},{8,9},{9,11},{10,8... | collective-permute-start | bytes 1179656 | tf_op jit(solution)/shard_map/ppermute | solution.py:78
  138.4 254.5 %reduce-scatter.2.cloned.1.call-start = ((), (), s32[]{:S(2)}) async-start(), calls=%async_computation.3 | async-start | bytes 7864320 | tf_op jit(solution)/shard_map/reduce_scatter | solution.py:127
  138.5 12.8 %collective-permute-start.11 = (bf16[48,768]{1,0:T(8,128)(2,1)S(1)}, bf16[48,768]{1,0:T(8,128)(2,1)S(1)}, u32[]{:S(2)}, u32[]{:S(2)}) collective-permute-start(bf16[48,768]{1,0:T(8,128)(2,1)S(1)} %copy-done.95), channel_id=1, source_target_pairs={{0,64},{4,68},{8,72},{12,76},{16,80},{20,84},{24,88},{28,92},{32,9... | collective-permute-start | bytes 221192 | tf_op jit(solution)/shard_map/ppermute | solution.py:22
  175.2 19.2 %collective-permute-start.9 = (bf16[384,768]{1,0:T(8,128)(2,1)S(1)}, bf16[384,768]{1,0:T(8,128)(2,1)}, u32[]{:S(2)}, u32[]{:S(2)}) collective-permute-start(bf16[384,768]{1,0:T(8,128)(2,1)S(1)} %fusion.81), channel_id=1, source_target_pairs={{0,4},{4,0},{8,12},{12,8},{16,20},{20,16},{24,28},{28,24},{32,36},... | collective-permute-start | bytes 1769480 | tf_op jit(solution)/shard_map/ppermute | solution.py:22
  179.2 40.5 %collective-permute-start.15 = (bf16[768,768]{1,0:T(8,128)(2,1)S(1)}, bf16[768,768]{1,0:T(8,128)(2,1)}, u32[]{:S(2)}, u32[]{:S(2)}) collective-permute-start(bf16[768,768]{1,0:T(8,128)(2,1)S(1)} %fusion.72), channel_id=1, source_target_pairs={{0,4},{4,0},{8,12},{12,8},{16,20},{20,16},{24,28},{28,24},{32,36},... | collective-permute-start | bytes 3538952 | tf_op jit(solution)/shard_map/ppermute | solution.py:22
  198.1 27.9 %collective-permute-start.10 = (bf16[768,768]{1,0:T(8,128)(2,1)}, bf16[768,768]{1,0:T(8,128)(2,1)}, u32[]{:S(2)}, u32[]{:S(2)}) collective-permute-start(bf16[768,768]{1,0:T(8,128)(2,1)} %fusion.74), channel_id=1, source_target_pairs={{0,8},{4,12},{8,0},{12,4},{16,24},{20,28},{24,16},{28,20},{32,40},... | collective-permute-start | bytes 3538952 | tf_op jit(solution)/shard_map/ppermute | solution.py:22
  257.5 49.6 %collective-permute-start.25 = (f32[768,768]{1,0:T(8,128)}, f32[768,768]{1,0:T(8,128)}, u32[]{:S(2)}, u32[]{:S(2)}) collective-permute-start(f32[768,768]{1,0:T(8,128)} %constant_dynamic-slice_fusion.4), channel_id=1, source_target_pairs={{0,8},{4,12},{8,0},{12,4},{16,24},{20,28},{24,16},{28,20},{32,40},... | collective-permute-start | bytes 7077896 | tf_op jit(solution)/shard_map/ppermute | solution.py:22
  267.4 83.5 %collective-permute-start.20 = (f32[768,768]{1,0:T(8,128)}, f32[768,768]{1,0:T(8,128)}, u32[]{:S(2)}, u32[]{:S(2)}) collective-permute-start(f32[768,768]{1,0:T(8,128)} %constant_dynamic-slice_fusion.9), channel_id=1, source_target_pairs={{0,4},{4,0},{8,12},{12,8},{16,20},{20,16},{24,28},{28,24},{32,36},... | collective-permute-start | bytes 7077896 | tf_op jit(solution)/shard_map/ppermute | solution.py:22
  312.4 63.8 %collective-permute-start.26 = (f32[384,768]{1,0:T(8,128)}, f32[384,768]{1,0:T(8,128)}, u32[]{:S(2)}, u32[]{:S(2)}) collective-permute-start(f32[384,768]{1,0:T(8,128)} %constant_dynamic-slice_fusion.3), channel_id=1, source_target_pairs={{0,4},{4,0},{8,12},{12,8},{16,20},{20,16},{24,28},{28,24},{32,36},... | collective-permute-start | bytes 3538952 | tf_op jit(solution)/shard_map/ppermute | solution.py:22
  355.1 28.5 %collective-permute-start.21 = (f32[384,768]{1,0:T(8,128)S(1)}, f32[384,768]{1,0:T(8,128)}, u32[]{:S(2)}, u32[]{:S(2)}) collective-permute-start(f32[384,768]{1,0:T(8,128)S(1)} %constant_dynamic-slice_fusion.8), channel_id=1, source_target_pairs={{0,8},{4,12},{8,0},{12,4},{16,24},{20,28},{24,16},{28,20},{32,40},... | collective-permute-start | bytes 3538952 | tf_op jit(solution)/shard_map/ppermute | solution.py:22
  379.9 11.1 %collective-permute-start.27 = (f32[192,768]{1,0:T(8,128)}, f32[192,768]{1,0:T(8,128)}, u32[]{:S(2)}, u32[]{:S(2)}) collective-permute-start(f32[192,768]{1,0:T(8,128)} %constant_dynamic-slice_fusion.2), channel_id=1, source_target_pairs={{0,32},{4,36},{8,40},{12,44},{16,48},{20,52},{24,56},{28,60},{32,0... | collective-permute-start | bytes 1769480 | tf_op jit(solution)/shard_map/ppermute | solution.py:22
  386.0 76.0 %collective-permute-start.22 = (f32[192,768]{1,0:T(8,128)}, f32[192,768]{1,0:T(8,128)}, u32[]{:S(2)}, u32[]{:S(2)}) collective-permute-start(f32[192,768]{1,0:T(8,128)} %constant_dynamic-slice_fusion.7), channel_id=1, source_target_pairs={{0,32},{4,36},{8,40},{12,44},{16,48},{20,52},{24,56},{28,60},{32,0... | collective-permute-start | bytes 1769480 | tf_op jit(solution)/shard_map/ppermute | solution.py:22
  442.4 20.7 %collective-permute-start.30 = (f32[7,7,1536]{2,1,0:T(8,128)S(1)}, f32[7,7,1536]{2,1,0:T(8,128)S(1)}, u32[]{:S(2)}, u32[]{:S(2)}) collective-permute-start(f32[7,7,1536]{2,1,0:T(8,128)S(1)} %bitcast_dynamic-update-slice_fusion), channel_id=1, source_target_pairs={{0,1},{1,0},{2,3},{3,2},{4,5},{5,4},{6,7},{7,6},{8,9},{9,8},{10,11... | collective-permute-start | bytes 903176 | tf_op jit(solution)/shard_map/ppermute | solution.py:22
  452.8 78.3 %collective-permute-start.16 = (f32[2,3,32,1536]{3,0,2,1:T(2,128)S(1)}, f32[2,3,32,1536]{3,0,2,1:T(2,128)S(1)}, u32[]{:S(2)}, u32[]{:S(2)}) collective-permute-start(f32[2,3,32,1536]{3,0,2,1:T(2,128)S(1)} %get-tuple-element.119), channel_id=1, source_target_pairs={{0,4},{4,8},{8,12},{12,16},{16,20},{20,24},{24,28},{28,32},{32,36}... | collective-permute-start | bytes 3538952 | tf_op jit(solution)/shard_map/ppermute | solution.py:14
  454.8 76.3 %collective-permute-start.17 = (f32[2,3,32,1536]{3,0,2,1:T(2,128)S(1)}, f32[2,3,32,1536]{3,0,2,1:T(2,128)S(1)}, u32[]{:S(2)}, u32[]{:S(2)}) collective-permute-start(f32[2,3,32,1536]{3,0,2,1:T(2,128)S(1)} %get-tuple-element.120), channel_id=1, source_target_pairs={{4,0},{8,4},{12,8},{16,12},{20,16},{24,20},{28,24},{32,28},{36,32}... | collective-permute-start | bytes 3538952 | tf_op jit(solution)/shard_map/ppermute | solution.py:15
  456.1 12.7 %collective-permute-start.28 = (f32[96,768]{1,0:T(8,128)S(1)}, f32[96,768]{1,0:T(8,128)S(1)}, u32[]{:S(2)}, u32[]{:S(2)}) collective-permute-start(f32[96,768]{1,0:T(8,128)S(1)} %constant_dynamic-slice_fusion.1), channel_id=1, source_target_pairs={{0,16},{4,20},{8,24},{12,28},{16,0},{20,4},{24,8},{28,12},{32,48},... | collective-permute-start | bytes 884744 | tf_op jit(solution)/shard_map/ppermute | solution.py:22
  463.2 54.3 %collective-permute-start.31 = (f32[7,7,1536]{2,1,0:T(8,128)S(1)}, f32[7,7,1536]{2,1,0:T(8,128)S(1)}, u32[]{:S(2)}, u32[]{:S(2)}) collective-permute-start(f32[7,7,1536]{2,1,0:T(8,128)S(1)} %add.589), channel_id=1, source_target_pairs={{0,2},{1,3},{2,0},{3,1},{4,6},{5,7},{6,4},{7,5},{8,10},{9,11},{10,... | collective-permute-start | bytes 903176 | tf_op jit(solution)/shard_map/ppermute | solution.py:22
  466.6 56.8 %collective-permute-start.23 = (f32[96,768]{1,0:T(8,128)S(1)}, f32[96,768]{1,0:T(8,128)S(1)}, u32[]{:S(2)}, u32[]{:S(2)}) collective-permute-start(f32[96,768]{1,0:T(8,128)S(1)} %constant_dynamic-slice_fusion.6), channel_id=1, source_target_pairs={{0,16},{4,20},{8,24},{12,28},{16,0},{20,4},{24,8},{28,12},{32,48},... | collective-permute-start | bytes 884744 | tf_op jit(solution)/shard_map/ppermute | solution.py:22
  517.7 21.1 %collective-permute-start.29 = (f32[48,768]{1,0:T(8,128)S(1)}, f32[48,768]{1,0:T(8,128)S(1)}, u32[]{:S(2)}, u32[]{:S(2)}) collective-permute-start(f32[48,768]{1,0:T(8,128)S(1)} %constant_dynamic-slice_fusion), channel_id=1, source_target_pairs={{0,64},{4,68},{8,72},{12,76},{16,80},{20,84},{24,88},{28,92},{32,9... | collective-permute-start | bytes 442376 | tf_op jit(solution)/shard_map/ppermute | solution.py:22
  526.4 12.2 %collective-permute-start.33 = (f32[7,7,1536]{2,1,0:T(8,128)S(1)}, f32[7,7,1536]{2,1,0:T(8,128)S(1)}, u32[]{:S(2)}, u32[]{:S(2)}) collective-permute-start(f32[7,7,1536]{2,1,0:T(8,128)S(1)} %add.591), channel_id=1, source_target_pairs={{0,8},{4,12},{8,0},{12,4},{16,24},{20,28},{24,16},{28,20},{32,40},... | collective-permute-start | bytes 903176 | tf_op jit(solution)/shard_map/ppermute | solution.py:22
  528.1 11.3 %collective-permute-start.24 = (f32[48,768]{1,0:T(8,128)S(1)}, f32[48,768]{1,0:T(8,128)S(1)}, u32[]{:S(2)}, u32[]{:S(2)}) collective-permute-start(f32[48,768]{1,0:T(8,128)S(1)} %constant_dynamic-slice_fusion.5), channel_id=1, source_target_pairs={{0,64},{4,68},{8,72},{12,76},{16,80},{20,84},{24,88},{28,92},{32,9... | collective-permute-start | bytes 442376 | tf_op jit(solution)/shard_map/ppermute | solution.py:22
  531.5 19.6 %collective-permute-start.18 = (f32[2,10,3,1536]{3,0,2,1:T(2,128)S(1)}, f32[2,10,3,1536]{3,0,2,1:T(2,128)S(1)}, u32[]{:S(2)}, u32[]{:S(2)}) collective-permute-start(f32[2,10,3,1536]{3,0,2,1:T(2,128)S(1)} %get-tuple-element.115), channel_id=1, source_target_pairs={{1,0},{2,1},{3,2},{5,4},{6,5},{7,6},{9,8},{10,9},{11,10},{13,12},{... | collective-permute-start | bytes 1105928 | tf_op jit(solution)/shard_map/ppermute | solution.py:15
  535.1 16.0 %collective-permute-start.19 = (f32[2,10,3,1536]{3,0,2,1:T(2,128)S(1)}, f32[2,10,3,1536]{3,0,2,1:T(2,128)S(1)}, u32[]{:S(2)}, u32[]{:S(2)}) collective-permute-start(f32[2,10,3,1536]{3,0,2,1:T(2,128)S(1)} %get-tuple-element.116), channel_id=1, source_target_pairs={{0,1},{1,2},{2,3},{4,5},{5,6},{6,7},{8,9},{9,10},{10,11},{12,13},{... | collective-permute-start | bytes 1105928 | tf_op jit(solution)/shard_map/ppermute | solution.py:14
  538.6 9.6 %collective-permute-start.34 = (f32[7,7,1536]{2,1,0:T(8,128)S(1)}, f32[7,7,1536]{2,1,0:T(8,128)S(1)}, u32[]{:S(2)}, u32[]{:S(2)}) collective-permute-start(f32[7,7,1536]{2,1,0:T(8,128)S(1)} %add.592), channel_id=1, source_target_pairs={{0,32},{4,36},{8,40},{12,44},{16,48},{20,52},{24,56},{28,60},{32,0... | collective-permute-start | bytes 903176 | tf_op jit(solution)/shard_map/ppermute | solution.py:22
  548.6 10.8 %collective-permute-start.35 = (f32[7,7,1536]{2,1,0:T(8,128)S(1)}, f32[7,7,1536]{2,1,0:T(8,128)S(1)}, u32[]{:S(2)}, u32[]{:S(2)}) collective-permute-start(f32[7,7,1536]{2,1,0:T(8,128)S(1)} %add.593), channel_id=1, source_target_pairs={{0,16},{4,20},{8,24},{12,28},{16,0},{20,4},{24,8},{28,12},{32,48},... | collective-permute-start | bytes 903176 | tf_op jit(solution)/shard_map/ppermute | solution.py:22
  559.5 40.2 %collective-permute-start.36 = (f32[7,7,1536]{2,1,0:T(8,128)S(1)}, f32[7,7,1536]{2,1,0:T(8,128)S(1)}, u32[]{:S(2)}, u32[]{:S(2)}) collective-permute-start(f32[7,7,1536]{2,1,0:T(8,128)S(1)} %add.594), channel_id=1, source_target_pairs={{0,64},{4,68},{8,72},{12,76},{16,80},{20,84},{24,88},{28,92},{32,9... | collective-permute-start | bytes 903176 | tf_op jit(solution)/shard_map/ppermute | solution.py:22
  (109 other events, 1670.8 us)
Sparse Core Ops, SparseCore 0:
  119.5 33.9 all-gather.4
  155.2 41.1 all-gather.2
  250.0 103.5 reduce-scatter.1

commit v2 on v1

--- a/solution.py
+++ b/solution.py
@@ -83,14 +83,28 @@
     out_grad = out_grad.transpose(0, 1, 3, 2, 4, 5).reshape(
         images, tile_rows, tile_cols, channel_total
     )
-    padded = with_halo(block_input, (("rows", 1), ("cols", 2)), kernel_reach)
-    padded = padded.astype(jnp.float32)
-    conv_out = jnp.zeros((images, tile_rows, tile_cols, channel_total), jnp.float32)
+    lane = 128
+    groups = channel_total // lane
+
+    def to_tiles(x):
+        x = x.reshape(images, tile_rows, tile_cols, groups, lane).transpose(1, 2, 0, 3, 4)
+        return x.reshape(tile_rows, tile_cols, images * groups, lane)
+
+    def from_tiles(t):
+        t = t.reshape(tile_rows, tile_cols, images, groups, lane).transpose(2, 0, 1, 3, 4)
+        return t.reshape(images, tile_rows, tile_cols, channel_total)
+
+    taps = jnp.tile(
+        conv_kernel.reshape(kernel_size, kernel_size, 1, groups, lane), (1, 1, images, 1, 1)
+    ).reshape(kernel_size, kernel_size, images * groups, lane)
+    padded = with_halo(to_tiles(block_input), (("rows", 0), ("cols", 1)), kernel_reach)
+    conv_t = jnp.zeros((tile_rows, tile_cols, images * groups, lane), jnp.float32)
     for r in range(kernel_size):
         for s in range(kernel_size):
-            conv_out = (
-                conv_out + conv_kernel[r, s] * padded[:, r : r + tile_rows, s : s + tile_cols]
+            conv_t = conv_t + taps[r, s] * padded[r : r + tile_rows, s : s + tile_cols].astype(
+                jnp.float32
             )
+    conv_out = from_tiles(conv_t)
     mean_val = jnp.mean(conv_out, axis=-1, keepdims=True)
     centered_input = conv_out - mean_val
     var_val = jnp.mean(centered_input * centered_input, axis=-1, keepdims=True)
@@ -124,13 +138,12 @@
     )
     grad_w1 = scatter_rows(in_terms, "rows", (0, 1, 3, 2, 4)) * scale
     grad_w2 = (scatter_rows(out_terms_t, "rows", (1, 0, 3, 2, 4)) * scale).T
-    normed_grad = lax.psum_scatter(
+    normed_grad = scatter_rows(
         lax.dot_general(
             hidden_grad, w_in_cols, (((1,), (1,)), ((), ())), preferred_element_type=jnp.float32
         ),
         "cols",
-        scatter_dimension=0,
-        tiled=True,
+        (0, 1)[:col_bits],
     )
     gain_applied = (
         normed_grad.reshape(images, tile_rows, tile_cols, channel_total) * layer_norm_gain
@@ -140,16 +153,16 @@
         - jnp.mean(gain_applied, axis=-1, keepdims=True)
         - standardized_input * jnp.mean(gain_applied * standardized_input, axis=-1, keepdims=True)
     )
+    grad_t = to_tiles(convolution_gradient)
     kernel_rows = []
     for r in range(kernel_size):
         row_terms = []
         for s in range(kernel_size):
-            row_terms.append(
-                jnp.sum(
-                    convolution_gradient * padded[:, r : r + tile_rows, s : s + tile_cols],
-                    axis=(0, 1, 2),
-                )
+            term = jnp.sum(
+                grad_t * padded[r : r + tile_rows, s : s + tile_cols].astype(jnp.float32),
+                axis=(0, 1),
             )
+            row_terms.append(term.reshape(images, channel_total).sum(axis=0))
         kernel_rows.append(jnp.stack(row_terms))
     grad_kernel = jnp.stack(kernel_rows)
     for bit in range(col_bits):
@@ -157,17 +170,18 @@
     for bit in (0, 1, 3, 2, 4)[:row_bits]:
         grad_kernel = grad_kernel + swap_with(grad_kernel, "rows", bit)
     grad_kernel = grad_kernel * scale
-    grad_pad = with_halo(convolution_gradient, (("rows", 1), ("cols", 2)), kernel_reach)
-    total = out_grad.astype(jnp.float32)
+    grad_pad = with_halo(grad_t, (("rows", 0), ("cols", 1)), kernel_reach)
+    total = to_tiles(out_grad).astype(jnp.float32)
     for r in range(kernel_size):
         for s in range(kernel_size):
             row_from = 2 * kernel_reach - r
             col_from = 2 * kernel_reach - s
             total = (
                 total
-                + conv_kernel[r, s]
-                * grad_pad[:, row_from : row_from + tile_rows, col_from : col_from + tile_cols]
+                + taps[r, s]
+                * grad_pad[row_from : row_from + tile_rows, col_from : col_from + tile_cols]
             )
+    total = from_tiles(total)
     input_grad = total.astype(jnp.bfloat16)
     return (input_grad, grad_w1, grad_w2, grad_kernel)
 

time: 612 us -> 584 us (0.954)
  local copies, waits for them, and re-layouts: 37.8 us -> 92.7 us
  other arithmetic: 186 us -> 138 us
  waiting for transfers between devices: 261 us -> 234 us
  starting transfers between devices: 79.6 us -> 70.5 us
    reduce_sum x1, other arithmetic: 56.1 us -> 1.42 us  [local(): mean_val = jnp.mean(conv_out, axis=-1, keepdims=True)]
    ppermute x27 -> x29, waiting for transfers between devices: 224 us -> 196 us  [swap_with(): return lax.ppermute(value, axis, [(i, i ^ 1 << bit) for i in range(peers)])]
    reshape x0 -> x51, local copies, waits for them, and re-layouts: none -> 27.6 us  [the longest x48 21 us: local(): row_terms.append(term.reshape(images, channel_total).sum(axis=0))]
    reduce_sum x4 -> x52, other arithmetic: 46.4 us -> 23.1 us  [the longest x3 16.2 us: local(): jnp.sum(grad_t * padded[r:r + tile_rows, s:s + tile_cols].astype(jnp.floa...]
    add x0 -> x1, other arithmetic: none -> 15.1 us  [local(): conv_t + taps[r, s] * padded[r:r + tile_rows, s:s + tile_cols].astype(jnp...]
    ppermute x27 -> x29, starting transfers between devices: 52.3 us -> 41.9 us  [swap_with(): return lax.ppermute(value, axis, [(i, i ^ 1 << bit) for i in range(peers)])]
    ppermute x4, waiting for transfers between devices: 5 us -> 15.2 us  [with_halo(): after = lax.ppermute(first, axis, down)]
    convert_element_type x5 -> x7, local copies, waits for them, and re-layouts: 8.38 us -> 17.9 us  [the longest x4 13 us: local(): total = to_tiles(out_grad).astype(jnp.float32)]
  transfers between devices with their start and end apart: 40 -> 41, of which waited for: 20 -> 21; matrix products, arithmetic and copies ran while one was open for 27% -> 34% of each run, Pallas kernels for 0% -> 0%
where the time goes in v2:
time: 584 us; the launch traced here: 573 us
  waiting for transfers between devices  234 us (40%)
  other arithmetic  138 us (24%)
  local copies, waits for them, and re-layouts  92.7 us (16%)
  starting transfers between devices  70.5 us (12%)
  matrix products  21.1 us (4%)
  between operations  17 us (3%)
    ppermute x29, waiting for transfers between devices, swap_with(): return lax.ppermute(value, axis, [(i, i ^ 1 << bit) for i in range(peers)])  196 us
    ppermute x29, starting transfers between devices, swap_with(): return lax.ppermute(value, axis, [(i, i ^ 1 << bit) for i in range(peers)])  41.9 us
    convert_element_type x1, other arithmetic, local(): input_grad = total.astype(jnp.bfloat16)  31.9 us
    concatenate x10, other arithmetic, gather_rows(): both = jnp.concatenate([value, other, value], axis=0)  24.7 us
    reshape x48, local copies, waits for them, and re-layouts, local(): row_terms.append(term.reshape(images, channel_total).sum(axis=0))  21 us
    ppermute x4, starting transfers between devices, with_halo(): before = lax.ppermute(last, axis, up)  18 us
    unnamed x219, local copies, waits for them, and re-layouts  16.9 us
    reduce_sum x3, other arithmetic, local(): jnp.sum(grad_t * padded[r:r + tile_rows, s:s + tile_cols].astype(jnp.floa...  16.2 us
  transfers between devices with their start and end apart: 41, of which 21 were waited for; matrix products, arithmetic and copies ran while one was open for 34% of the time, Pallas kernels for 0%

profile of v2, /device:TPU:1, one launch (start us, length us, event | category | flops | bytes accessed | tf_op | source)
XLA Modules:
  0.0 573.5 jit_solution(14143562612650487871)
XLA Ops:
  10.8 5.0 collective-permute-start.2
  17.4 9.3 %collective-permute-done.3 = bf16[3,32,24,128]{3,1,2,0:T(8,128)(2,1)S(1)} collective-permute-done((bf16[3,32,24,128]{3,1,2,0:T(8,128)(2,1)S(1)}, bf16[3,32,24,128]{3,1,2,0:T(8,128)(2,1)S(1)}, u32[]{:S(2)}, u32[]{:S(2)}) %collective-permute-start.3) | collective-permute-done | bytes 589856 | tf_op jit(solution)/shard_map/ppermute | solution.py:15
  26.7 13.5 %collective-permute-done.2 = bf16[3,32,24,128]{3,1,2,0:T(8,128)(2,1)S(1)} collective-permute-done((bf16[3,32,24,128]{3,1,2,0:T(8,128)(2,1)S(1)}, bf16[3,32,24,128]{3,1,2,0:T(8,128)(2,1)S(1)}, u32[]{:S(2)}, u32[]{:S(2)}) %collective-permute-start.2) | collective-permute-done | bytes 589856 | tf_op jit(solution)/shard_map/ppermute | solution.py:14
  40.4 5.6 collective-permute-start.4
  49.2 5.9 %collective-permute-done.5 = bf16[10,3,24,128]{3,1,2,0:T(4,128)(2,1)S(1)} collective-permute-done((bf16[10,3,24,128]{3,1,2,0:T(4,128)(2,1)S(1)}, bf16[10,3,24,128]{3,1,2,0:T(4,128)(2,1)S(1)}, u32[]{:S(2)}, u32[]{:S(2)}) %collective-permute-start.5) | collective-permute-done | bytes 184352 | tf_op jit(solution)/shard_map/ppermute | solution.py:15
  57.0 15.1 %fusion.82 = f32[4,32,24,128]{3,1,2,0:T(8,128)S(1)} fusion(bf16[4,32,24,128]{3,1,2,0:T(8,128)(2,1)S(1)} %bitcast.172, f32[24,128]{1,0:T(8,128)S(1)} %bitcast.262, f32[24,128]{1,0:T(8,128)S(1)} %bitcast.264, f32[24,128]{1,0:T(8,128)S(1)} %bitcast.266, f32[24,128]{1,0:T(8,128)S(1)} %bitcast.268, f32[24,128]{1,0:T(8,128)S(1)} %bitcast.270, ...), kind=kLoop, calls=%fused_computation.218 | loop fusion | flops 59768832 | bytes 37171200 | tf_op jit(solution)/shard_map/add | solution.py:104
  94.2 5.9 %collective-permute-done = bf16[2,16,6144]{2,1,0:T(8,128)(2,1)} collective-permute-done((bf16[2,16,6144]{2,1,0:T(8,128)(2,1)}, bf16[2,16,6144]{2,1,0:T(8,128)(2,1)}, u32[]{:S(2)}, u32[]{:S(2)}) %collective-permute-start) | collective-permute-done | bytes 393248 | tf_op jit(solution)/shard_map/ppermute | solution.py:77
  134.7 3.6 collective-permute-done.12
  143.5 4.8 collective-permute-done.13
  151.1 14.1 %collective-permute-done.9 = bf16[384,768]{1,0:T(8,128)(2,1)} collective-permute-done((bf16[384,768]{1,0:T(8,128)(2,1)}, bf16[384,768]{1,0:T(8,128)(2,1)}, u32[]{:S(2)}, u32[]{:S(2)}) %collective-permute-start.9) | collective-permute-done | bytes 589856 | tf_op jit(solution)/shard_map/ppermute | solution.py:22
  173.7 22.4 %collective-permute-done.10 = bf16[768,768]{1,0:T(8,128)(2,1)} collective-permute-done((bf16[768,768]{1,0:T(8,128)(2,1)}, bf16[768,768]{1,0:T(8,128)(2,1)}, u32[]{:S(2)}, u32[]{:S(2)}) %collective-permute-start.10) | collective-permute-done | bytes 1179680 | tf_op jit(solution)/shard_map/ppermute | solution.py:22
  196.0 3.8 fusion.9
  201.5 3.8 fusion.7
  206.9 6.9 %fusion.196 = f32[1024,768]{1,0:T(8,128)} fusion(bf16[1024,1536]{1,0:T(8,128)(2,1)} %all-gather.5.cloned.1.call-done, bf16[1536,768]{1,0:T(8,128)(2,1)} %bitcast.192), kind=kOutput, calls=%fused_computation.450 | convolution fusion | flops 2415919104 | bytes 8650752 | tf_op jit(solution)/shard_map/dot_general | solution.py:126
  213.8 5.6 fusion.106
  243.3 32.6 %collective-permute-done.27 = f32[768,768]{1,0:T(8,128)} collective-permute-done((f32[768,768]{1,0:T(8,128)}, f32[768,768]{1,0:T(8,128)}, u32[]{:S(2)}, u32[]{:S(2)}) %collective-permute-start.27) | collective-permute-done | bytes 2359328 | tf_op jit(solution)/shard_map/ppermute | solution.py:22
  281.7 14.7 %collective-permute-done.22 = f32[768,768]{1,0:T(8,128)} collective-permute-done((f32[768,768]{1,0:T(8,128)}, f32[768,768]{1,0:T(8,128)}, u32[]{:S(2)}, u32[]{:S(2)}) %collective-permute-start.22) | collective-permute-done | bytes 2359328 | tf_op jit(solution)/shard_map/ppermute | solution.py:22
  305.5 16.2 %collective-permute-done.28 = f32[384,768]{1,0:T(8,128)} collective-permute-done((f32[384,768]{1,0:T(8,128)}, f32[384,768]{1,0:T(8,128)}, u32[]{:S(2)}, u32[]{:S(2)}) %collective-permute-start.28) | collective-permute-done | bytes 1179680 | tf_op jit(solution)/shard_map/ppermute | solution.py:22
  341.4 12.4 %collective-permute-done.17 = f32[256,1536]{1,0:T(8,128)} collective-permute-done((f32[256,1536]{1,0:T(8,128)}, f32[256,1536]{1,0:T(8,128)}, u32[]{:S(2)}, u32[]{:S(2)}) %collective-permute-start.17) | collective-permute-done | bytes 1572896 | tf_op jit(solution)/shard_map/ppermute | solution.py:22
  367.9 5.0 fusion.101
  372.9 5.2 fusion.105
  386.5 6.1 %fusion.102 = (f32[24,128]{1,0:T(8,128)}, f32[24,128]{1,0:T(8,128)}, f32[24,128]{1,0:T(8,128)}, f32[24,128]{1,0:T(8,128)}, f32[24,128]{1,0:T(8,128)}, /*index=5*...) fusion(f32[4,32,24,128]{3,1,2,0:T(8,128)} %bitcast.156, ...), kind=kLoop, calls=%fused_computation.238 | loop fusion | flops 16478208 | bytes 8404992 | tf_op jit(solution)/shard_map/reduce_sum | solution.py:161
  421.5 4.1 collective-permute-start.18
  429.6 3.5 collective-permute-start.33
  434.7 52.5 %collective-permute-done.33 = f32[7,7,1536]{2,1,0:T(8,128)S(1)} collective-permute-done((f32[7,7,1536]{2,1,0:T(8,128)S(1)}, f32[7,7,1536]{2,1,0:T(8,128)S(1)}, u32[]{:S(2)}, u32[]{:S(2)}) %collective-permute-start.33) | collective-permute-done | bytes 301088 | tf_op jit(solution)/shard_map/ppermute | solution.py:22
  490.3 6.3 %collective-permute-done.34 = f32[7,7,1536]{2,1,0:T(8,128)S(1)} collective-permute-done((f32[7,7,1536]{2,1,0:T(8,128)S(1)}, f32[7,7,1536]{2,1,0:T(8,128)S(1)}, u32[]{:S(2)}, u32[]{:S(2)}) %collective-permute-start.34) | collective-permute-done | bytes 301088 | tf_op jit(solution)/shard_map/ppermute | solution.py:22
  501.0 3.8 collective-permute-start.20
  509.7 8.0 %collective-permute-done.36 = f32[7,7,1536]{2,1,0:T(8,128)S(1)} collective-permute-done((f32[7,7,1536]{2,1,0:T(8,128)S(1)}, f32[7,7,1536]{2,1,0:T(8,128)S(1)}, u32[]{:S(2)}, u32[]{:S(2)}) %collective-permute-start.36) | collective-permute-done | bytes 301088 | tf_op jit(solution)/shard_map/ppermute | solution.py:22
  518.0 3.6 collective-permute-start.37
  521.6 4.4 pad_maximum_fusion
  526.0 3.6 collective-permute-done.37
  530.7 31.9 %fusion.167 = bf16[4,32,24,128]{3,1,2,0:T(8,128)(2,1)S(1)} fusion(f32[10,35,24,128]{3,1,2,0:T(8,128)} %get-tuple-element.67, f32[4,32,24,128]{3,1,2,0:T(8,128)S(1)} %bitcast.159, f32[3,32,24,128]{3,1,2,0:T(8,128)S(1)} %collective-permute-done.18, f32[10,35,24,128]{3,1,2,0:T(8,128)} %get-tuple-element.66, f32[3,32,24,128]{3,1,2,0:T(8,128)S(1)} %collective-permute-done.19, ...), kind=kLoop, calls=%fused_computation.352 | loop fusion | flops 41287680 | bytes 72953856 | tf_op jit(solution)/shard_map/convert_element_type | solution.py:185
  (520 shorter events, 217.4 us)
Async XLA Ops:
  7.2 199.8 %all-gather.5.cloned.1.call-start = ((), (), s32[]{:S(2)}) async-start(), calls=%async_computation.1 | async-start | bytes 3932160 | tf_op jit(solution)/shard_map/all_gather | solution.py:125
  9.3 17.4 %collective-permute-start.3 = (bf16[3,32,24,128]{3,1,2,0:T(8,128)(2,1)S(1)}, bf16[3,32,24,128]{3,1,2,0:T(8,128)(2,1)S(1)}, u32[]{:S(2)}, u32[]{:S(2)}) collective-permute-start(bf16[3,32,24,128]{3,1,2,0:T(8,128)(2,1)S(1)} %bitcast.197), channel_id=1, source_target_pairs={{4,0},{8,4},{12,8},{16,12},{20,16},{24,20},{28,24},{32,28},{36,32}... | collective-permute-start | bytes 1769480 | tf_op jit(solution)/shard_map/ppermute | solution.py:15
  10.8 29.5 %collective-permute-start.2 = (bf16[3,32,24,128]{3,1,2,0:T(8,128)(2,1)S(1)}, bf16[3,32,24,128]{3,1,2,0:T(8,128)(2,1)S(1)}, u32[]{:S(2)}, u32[]{:S(2)}) collective-permute-start(bf16[3,32,24,128]{3,1,2,0:T(8,128)(2,1)S(1)} %bitcast.198), channel_id=1, source_target_pairs={{0,4},{4,8},{8,12},{12,16},{16,20},{20,24},{24,28},{28,32},{32,36}... | collective-permute-start | bytes 1769480 | tf_op jit(solution)/shard_map/ppermute | solution.py:14
  87.0 126.9 %all-gather.3.cloned.1.call-start = ((), (), s32[]{:S(2)}) async-start(), calls=%async_computation | async-start | bytes 3932160 | tf_op jit(solution)/shard_map/all_gather | solution.py:124
  89.2 10.9 %collective-permute-start = (bf16[2,16,6144]{2,1,0:T(8,128)(2,1)}, bf16[2,16,6144]{2,1,0:T(8,128)(2,1)}, u32[]{:S(2)}, u32[]{:S(2)}) collective-permute-start(bf16[2,16,6144]{2,1,0:T(8,128)(2,1)} %get-tuple-element.79), channel_id=1, source_target_pairs={{0,0},{1,2},{2,1},{3,3},{4,4},{5,6},{6,5},{7,7},{8,8},{9,10},{10,9... | collective-permute-start | bytes 1179656 | tf_op jit(solution)/shard_map/ppermute | solution.py:77
  129.1 10.6 %collective-permute-start.8 = (bf16[192,768]{1,0:T(8,128)(2,1)}, bf16[192,768]{1,0:T(8,128)(2,1)}, u32[]{:S(2)}, u32[]{:S(2)}) collective-permute-start(bf16[192,768]{1,0:T(8,128)(2,1)} %fusion.186), channel_id=1, source_target_pairs={{0,32},{4,36},{8,40},{12,44},{16,48},{20,52},{24,56},{28,60},{32,0... | collective-permute-start | bytes 884744 | tf_op jit(solution)/shard_map/ppermute | solution.py:22
  142.0 23.2 %collective-permute-start.9 = (bf16[384,768]{1,0:T(8,128)(2,1)}, bf16[384,768]{1,0:T(8,128)(2,1)}, u32[]{:S(2)}, u32[]{:S(2)}) collective-permute-start(bf16[384,768]{1,0:T(8,128)(2,1)} %fusion.182), channel_id=1, source_target_pairs={{0,4},{4,0},{8,12},{12,8},{16,20},{20,16},{24,28},{28,24},{32,36},... | collective-permute-start | bytes 1769480 | tf_op jit(solution)/shard_map/ppermute | solution.py:22
  150.0 19.7 %collective-permute-start.14 = (bf16[384,768]{1,0:T(8,128)(2,1)}, bf16[384,768]{1,0:T(8,128)(2,1)}, u32[]{:S(2)}, u32[]{:S(2)}) collective-permute-start(bf16[384,768]{1,0:T(8,128)(2,1)} %fusion.180), channel_id=1, source_target_pairs={{0,8},{4,12},{8,0},{12,4},{16,24},{20,28},{24,16},{28,20},{32,40},... | collective-permute-start | bytes 1769480 | tf_op jit(solution)/shard_map/ppermute | solution.py:22
  168.6 27.5 %collective-permute-start.10 = (bf16[768,768]{1,0:T(8,128)(2,1)}, bf16[768,768]{1,0:T(8,128)(2,1)}, u32[]{:S(2)}, u32[]{:S(2)}) collective-permute-start(bf16[768,768]{1,0:T(8,128)(2,1)} %fusion.171), channel_id=1, source_target_pairs={{0,8},{4,12},{8,0},{12,4},{16,24},{20,28},{24,16},{28,20},{32,40},... | collective-permute-start | bytes 3538952 | tf_op jit(solution)/shard_map/ppermute | solution.py:22
  173.1 28.4 %collective-permute-start.15 = (bf16[768,768]{1,0:T(8,128)(2,1)}, bf16[768,768]{1,0:T(8,128)(2,1)}, u32[]{:S(2)}, u32[]{:S(2)}) collective-permute-start(bf16[768,768]{1,0:T(8,128)(2,1)} %fusion.169), channel_id=1, source_target_pairs={{0,4},{4,0},{8,12},{12,8},{16,20},{20,16},{24,28},{28,24},{32,36},... | collective-permute-start | bytes 3538952 | tf_op jit(solution)/shard_map/ppermute | solution.py:22
  223.4 52.5 %collective-permute-start.27 = (f32[768,768]{1,0:T(8,128)}, f32[768,768]{1,0:T(8,128)}, u32[]{:S(2)}, u32[]{:S(2)}) collective-permute-start(f32[768,768]{1,0:T(8,128)} %constant_dynamic-slice_fusion.4), channel_id=1, source_target_pairs={{0,8},{4,12},{8,0},{12,4},{16,24},{20,28},{24,16},{28,20},{32,40},... | collective-permute-start | bytes 7077896 | tf_op jit(solution)/shard_map/ppermute | solution.py:22
  236.0 64.9 %collective-permute-start.16 = (f32[512,1536]{1,0:T(8,128)}, f32[512,1536]{1,0:T(8,128)}, u32[]{:S(2)}, u32[]{:S(2)}) collective-permute-start(f32[512,1536]{1,0:T(8,128)} %constant_dynamic-slice_fusion.11), channel_id=1, source_target_pairs={{0,1},{1,0},{2,3},{3,2},{4,5},{5,4},{6,7},{7,6},{8,9},{9,8},{10,11... | collective-permute-start | bytes 9437192 | tf_op jit(solution)/shard_map/ppermute | solution.py:22
  243.3 53.1 %collective-permute-start.22 = (f32[768,768]{1,0:T(8,128)}, f32[768,768]{1,0:T(8,128)}, u32[]{:S(2)}, u32[]{:S(2)}) collective-permute-start(f32[768,768]{1,0:T(8,128)} %constant_dynamic-slice_fusion.9), channel_id=1, source_target_pairs={{0,4},{4,0},{8,12},{12,8},{16,20},{20,16},{24,28},{28,24},{32,36},... | collective-permute-start | bytes 7077896 | tf_op jit(solution)/shard_map/ppermute | solution.py:22
  281.3 40.4 %collective-permute-start.28 = (f32[384,768]{1,0:T(8,128)}, f32[384,768]{1,0:T(8,128)}, u32[]{:S(2)}, u32[]{:S(2)}) collective-permute-start(f32[384,768]{1,0:T(8,128)} %constant_dynamic-slice_fusion.3), channel_id=1, source_target_pairs={{0,4},{4,0},{8,12},{12,8},{16,20},{20,16},{24,28},{28,24},{32,36},... | collective-permute-start | bytes 3538952 | tf_op jit(solution)/shard_map/ppermute | solution.py:22
  299.7 34.0 %collective-permute-start.23 = (f32[384,768]{1,0:T(8,128)}, f32[384,768]{1,0:T(8,128)}, u32[]{:S(2)}, u32[]{:S(2)}) collective-permute-start(f32[384,768]{1,0:T(8,128)} %constant_dynamic-slice_fusion.8), channel_id=1, source_target_pairs={{0,8},{4,12},{8,0},{12,4},{16,24},{20,28},{24,16},{28,20},{32,40},... | collective-permute-start | bytes 3538952 | tf_op jit(solution)/shard_map/ppermute | solution.py:22
  305.5 48.3 %collective-permute-start.17 = (f32[256,1536]{1,0:T(8,128)}, f32[256,1536]{1,0:T(8,128)}, u32[]{:S(2)}, u32[]{:S(2)}) collective-permute-start(f32[256,1536]{1,0:T(8,128)} %constant_dynamic-slice_fusion.10), channel_id=1, source_target_pairs={{0,2},{1,3},{2,0},{3,1},{4,6},{5,7},{6,4},{7,5},{8,10},{9,11},{10,... | collective-permute-start | bytes 4718600 | tf_op jit(solution)/shard_map/ppermute | solution.py:22
  325.4 14.1 %collective-permute-start.29 = (f32[192,768]{1,0:T(8,128)}, f32[192,768]{1,0:T(8,128)}, u32[]{:S(2)}, u32[]{:S(2)}) collective-permute-start(f32[192,768]{1,0:T(8,128)} %constant_dynamic-slice_fusion.2), channel_id=1, source_target_pairs={{0,32},{4,36},{8,40},{12,44},{16,48},{20,52},{24,56},{28,60},{32,0... | collective-permute-start | bytes 1769480 | tf_op jit(solution)/shard_map/ppermute | solution.py:22
  337.2 95.9 %collective-permute-start.24 = (f32[192,768]{1,0:T(8,128)}, f32[192,768]{1,0:T(8,128)}, u32[]{:S(2)}, u32[]{:S(2)}) collective-permute-start(f32[192,768]{1,0:T(8,128)} %constant_dynamic-slice_fusion.7), channel_id=1, source_target_pairs={{0,32},{4,36},{8,40},{12,44},{16,48},{20,52},{24,56},{28,60},{32,0... | collective-permute-start | bytes 1769480 | tf_op jit(solution)/shard_map/ppermute | solution.py:22
  417.9 10.7 %collective-permute-start.32 = (f32[7,7,1536]{2,1,0:T(8,128)}, f32[7,7,1536]{2,1,0:T(8,128)S(1)}, u32[]{:S(2)}, u32[]{:S(2)}) collective-permute-start(f32[7,7,1536]{2,1,0:T(8,128)} %bitcast_dynamic-update-slice_fusion), channel_id=1, source_target_pairs={{0,1},{1,0},{2,3},{3,2},{4,5},{5,4},{6,7},{7,6},{8,9},{9,8},{10,11... | collective-permute-start | bytes 903176 | tf_op jit(solution)/shard_map/ppermute | solution.py:22
  420.1 80.7 %collective-permute-start.19 = (f32[3,32,24,128]{3,1,2,0:T(8,128)S(1)}, f32[3,32,24,128]{3,1,2,0:T(8,128)S(1)}, u32[]{:S(2)}, u32[]{:S(2)}) collective-permute-start(f32[3,32,24,128]{3,1,2,0:T(8,128)S(1)} %bitcast.195), channel_id=1, source_target_pairs={{4,0},{8,4},{12,8},{16,12},{20,16},{24,20},{28,24},{32,28},{36,32}... | collective-permute-start | bytes 3538952 | tf_op jit(solution)/shard_map/ppermute | solution.py:15
  421.5 79.3 %collective-permute-start.18 = (f32[3,32,24,128]{3,1,2,0:T(8,128)S(1)}, f32[3,32,24,128]{3,1,2,0:T(8,128)S(1)}, u32[]{:S(2)}, u32[]{:S(2)}) collective-permute-start(f32[3,32,24,128]{3,1,2,0:T(8,128)S(1)} %bitcast.194), channel_id=1, source_target_pairs={{0,4},{4,8},{8,12},{12,16},{16,20},{20,24},{24,28},{28,32},{32,36}... | collective-permute-start | bytes 3538952 | tf_op jit(solution)/shard_map/ppermute | solution.py:14
  425.6 61.8 %collective-permute-start.30 = (f32[96,768]{1,0:T(8,128)S(1)}, f32[96,768]{1,0:T(8,128)S(1)}, u32[]{:S(2)}, u32[]{:S(2)}) collective-permute-start(f32[96,768]{1,0:T(8,128)S(1)} %constant_dynamic-slice_fusion.1), channel_id=1, source_target_pairs={{0,16},{4,20},{8,24},{12,28},{16,0},{20,4},{24,8},{28,12},{32,48},... | collective-permute-start | bytes 884744 | tf_op jit(solution)/shard_map/ppermute | solution.py:22
  429.6 57.7 %collective-permute-start.33 = (f32[7,7,1536]{2,1,0:T(8,128)S(1)}, f32[7,7,1536]{2,1,0:T(8,128)S(1)}, u32[]{:S(2)}, u32[]{:S(2)}) collective-permute-start(f32[7,7,1536]{2,1,0:T(8,128)S(1)} %add.613), channel_id=1, source_target_pairs={{0,2},{1,3},{2,0},{3,1},{4,6},{5,7},{6,4},{7,5},{8,10},{9,11},{10,... | collective-permute-start | bytes 903176 | tf_op jit(solution)/shard_map/ppermute | solution.py:22
  434.3 63.6 %collective-permute-start.25 = (f32[96,768]{1,0:T(8,128)S(1)}, f32[96,768]{1,0:T(8,128)S(1)}, u32[]{:S(2)}, u32[]{:S(2)}) collective-permute-start(f32[96,768]{1,0:T(8,128)S(1)} %constant_dynamic-slice_fusion.6), channel_id=1, source_target_pairs={{0,16},{4,20},{8,24},{12,28},{16,0},{20,4},{24,8},{28,12},{32,48},... | collective-permute-start | bytes 884744 | tf_op jit(solution)/shard_map/ppermute | solution.py:22
  487.5 20.8 %collective-permute-start.31 = (f32[48,768]{1,0:T(8,128)S(1)}, f32[48,768]{1,0:T(8,128)S(1)}, u32[]{:S(2)}, u32[]{:S(2)}) collective-permute-start(f32[48,768]{1,0:T(8,128)S(1)} %constant_dynamic-slice_fusion), channel_id=1, source_target_pairs={{0,64},{4,68},{8,72},{12,76},{16,80},{20,84},{24,88},{28,92},{32,9... | collective-permute-start | bytes 442376 | tf_op jit(solution)/shard_map/ppermute | solution.py:22
  496.6 11.5 %collective-permute-start.35 = (f32[7,7,1536]{2,1,0:T(8,128)S(1)}, f32[7,7,1536]{2,1,0:T(8,128)S(1)}, u32[]{:S(2)}, u32[]{:S(2)}) collective-permute-start(f32[7,7,1536]{2,1,0:T(8,128)S(1)} %add.615), channel_id=1, source_target_pairs={{0,8},{4,12},{8,0},{12,4},{16,24},{20,28},{24,16},{28,20},{32,40},... | collective-permute-start | bytes 903176 | tf_op jit(solution)/shard_map/ppermute | solution.py:22
  498.0 11.0 %collective-permute-start.26 = (f32[48,768]{1,0:T(8,128)S(1)}, f32[48,768]{1,0:T(8,128)S(1)}, u32[]{:S(2)}, u32[]{:S(2)}) collective-permute-start(f32[48,768]{1,0:T(8,128)S(1)} %constant_dynamic-slice_fusion.5), channel_id=1, source_target_pairs={{0,64},{4,68},{8,72},{12,76},{16,80},{20,84},{24,88},{28,92},{32,9... | collective-permute-start | bytes 442376 | tf_op jit(solution)/shard_map/ppermute | solution.py:22
  501.0 20.5 %collective-permute-start.20 = (f32[10,3,24,128]{3,1,2,0:T(4,128)S(1)}, f32[10,3,24,128]{3,1,2,0:T(4,128)S(1)}, u32[]{:S(2)}, u32[]{:S(2)}) collective-permute-start(f32[10,3,24,128]{3,1,2,0:T(4,128)S(1)} %get-tuple-element.68), channel_id=1, source_target_pairs={{1,0},{2,1},{3,2},{5,4},{6,5},{7,6},{9,8},{10,9},{11,10},{13,12},{... | collective-permute-start | bytes 1105928 | tf_op jit(solution)/shard_map/ppermute | solution.py:15
  504.8 16.8 %collective-permute-start.21 = (f32[10,3,24,128]{3,1,2,0:T(4,128)S(1)}, f32[10,3,24,128]{3,1,2,0:T(4,128)S(1)}, u32[]{:S(2)}, u32[]{:S(2)}) collective-permute-start(f32[10,3,24,128]{3,1,2,0:T(4,128)S(1)} %get-tuple-element.69), channel_id=1, source_target_pairs={{0,1},{1,2},{2,3},{4,5},{5,6},{6,7},{8,9},{9,10},{10,11},{12,13},{... | collective-permute-start | bytes 1105928 | tf_op jit(solution)/shard_map/ppermute | solution.py:14
  508.2 9.5 %collective-permute-start.36 = (f32[7,7,1536]{2,1,0:T(8,128)S(1)}, f32[7,7,1536]{2,1,0:T(8,128)S(1)}, u32[]{:S(2)}, u32[]{:S(2)}) collective-permute-start(f32[7,7,1536]{2,1,0:T(8,128)S(1)} %add.616), channel_id=1, source_target_pairs={{0,32},{4,36},{8,40},{12,44},{16,48},{20,52},{24,56},{28,60},{32,0... | collective-permute-start | bytes 903176 | tf_op jit(solution)/shard_map/ppermute | solution.py:22
  518.0 11.6 %collective-permute-start.37 = (f32[7,7,1536]{2,1,0:T(8,128)S(1)}, f32[7,7,1536]{2,1,0:T(8,128)S(1)}, u32[]{:S(2)}, u32[]{:S(2)}) collective-permute-start(f32[7,7,1536]{2,1,0:T(8,128)S(1)} %add.617), channel_id=1, source_target_pairs={{0,16},{4,20},{8,24},{12,28},{16,0},{20,4},{24,8},{28,12},{32,48},... | collective-permute-start | bytes 903176 | tf_op jit(solution)/shard_map/ppermute | solution.py:22
  530.4 34.0 %collective-permute-start.38 = (f32[7,7,1536]{2,1,0:T(8,128)}, f32[7,7,1536]{2,1,0:T(8,128)}, u32[]{:S(2)}, u32[]{:S(2)}) collective-permute-start(f32[7,7,1536]{2,1,0:T(8,128)} %add.618), channel_id=1, source_target_pairs={{0,64},{4,68},{8,72},{12,76},{16,80},{20,84},{24,88},{28,92},{32,9... | collective-permute-start | bytes 903176 | tf_op jit(solution)/shard_map/ppermute | solution.py:22
  (115 other events, 2063.3 us)
Sparse Core Ops, SparseCore 0:
  87.1 33.9 all-gather.4
  122.8 40.6 all-gather.2
